TPU v7x, 768 devices: a whole 4x8x12 slice. The times are simulated.
768 devices in a mesh: ctx: 32 (over z_hi, y, core), tp: 24 (over z_lo, x).
Axes of the slice: x: 4, y: 8, z: 12 (z_hi: 2, z_lo: 6; z = z_hi * 6 + z_lo), core: 2. Of those that a mesh axis runs over, the one named last changes fastest.
Arguments:
- queries: bfloat16 [4096, 3072], P('ctx', 'tp'), may hold values from -40 to 40
- keys: bfloat16 [4096, 768], P('ctx'), may hold values from -6 to 6
- values: bfloat16 [4096, 768], P('ctx'), may hold values from -6 to 6
- roles: int32 [4096], P('ctx'), may hold values from 0 to 15
- role_table: float32 [24, 16, 16], P('tp'), may hold values from -4 to 4
- block_mask: int32 [32, 32], replicated, may hold values 0 or 1
- d_out: bfloat16 [4096, 3072], P('ctx', 'tp'), may hold values from -6 to 6
Outputs:
- attended: bfloat16 [4096, 3072], P('ctx', 'tp')
- d_queries: bfloat16 [4096, 3072], P('ctx', 'tp')
- d_keys: bfloat16 [4096, 768], P('ctx')
- d_values: bfloat16 [4096, 768], P('ctx')
All inputs are finite; a program needn't handle non-finite values.
Results may differ from a plain program's by a relative error of at most 0.034.
Values may be sent and summed in bfloat16 or wider, within the bound.
No kernel may reach another device: no remote copies, remote signals or barrier semaphores. Data moves between devices by JAX's collectives and lax.ppermute only.
A program may use at most 32 MiB of HBM per device.

v0:
```python
import math

import jax
import jax.numpy as jnp
from jax import lax
from jax.sharding import PartitionSpec as P

HS = 128
GROUP = 4
BLK = 128


def shifted(block, axis, distance):
    devices = range(lax.axis_size(axis))
    route = [(i - distance, i) for i in devices if i - distance in devices]
    return lax.ppermute(block, axis, route)


def passed_along(value, axis, steps):
    count = lax.axis_size(axis)
    pairs = [(source, (source + steps) % count) for source in range(count)]
    return lax.ppermute(value, axis, pairs)


def on_device(queries, keys, values, roles, role_table, block_mask, d_out):
    tok_rows = queries.shape[0]
    head_count = role_table.shape[0]
    role_count = role_table.shape[1]
    block_count = block_mask.shape[0]
    scale = 1.0 / math.sqrt(HS)
    kv_count = keys.shape[1] // HS
    first_head = lax.axis_index("tp") * head_count
    column = (first_head + 0) // GROUP
    own_keys = lax.dynamic_slice_in_dim(keys, column * HS, HS, 1)
    own_values = lax.dynamic_slice_in_dim(values, column * HS, HS, 1)
    owners = [column]
    kv_pair = jnp.stack([own_keys, own_values], axis=1)
    chooser = (jnp.stack(owners)[:, None] == jnp.arange(kv_count)[None, :]).astype(jnp.float32)
    all_roles = lax.all_gather(roles, "ctx", axis=0, tiled=True)
    query_pos = lax.axis_index("ctx") * tok_rows + jnp.arange(tok_rows)
    query_block = query_pos // BLK
    role_onehot = (roles[:, None] == jnp.arange(role_count)[None, :]).astype(jnp.float32)
    table_rows = jnp.einsum("sr,hrc->hsc", role_onehot, role_table, precision=lax.Precision.HIGHEST)
    block_onehot = (query_block[:, None] == jnp.arange(block_count)[None, :]).astype(jnp.float32)
    mask_rows = jnp.dot(
        block_onehot, block_mask.astype(jnp.float32), precision=lax.Precision.HIGHEST
    )
    query3 = queries.reshape(tok_rows, head_count, HS)
    grad3 = d_out.reshape(tok_rows, head_count, HS)
    ctx_count = lax.axis_size("ctx")
    factor = 1
    while ctx_count % (factor * 2) == 0 and factor * 2 * tok_rows <= 1024:
        factor = factor * 2

    def scores(piece, start):
        count = piece.shape[0]
        key3 = piece[:, 0].reshape(count, head_count, HS)
        value3 = piece[:, 1].reshape(count, head_count, HS)
        key_pos = start + jnp.arange(count)
        key_block = key_pos // BLK
        key_roles = lax.dynamic_slice_in_dim(all_roles, start, count)
        key_onehot = (key_roles[:, None] == jnp.arange(role_count)[None, :]).astype(jnp.float32)
        bias = jnp.einsum("hsc,nc->hsn", table_rows, key_onehot, precision=lax.Precision.HIGHEST)
        kblock_onehot = (key_block[:, None] == jnp.arange(block_count)[None, :]).astype(jnp.float32)
        block_open = jnp.dot(mask_rows, kblock_onehot.T, precision=lax.Precision.HIGHEST) > 0.5
        allowed = (key_pos[None, :] <= query_pos[:, None]) & (
            block_open | (key_block[None, :] == query_block[:, None])
        )
        score = (
            jnp.einsum("shd,nhd->hsn", query3, key3, preferred_element_type=jnp.float32) * scale
            + bias
        )
        score = jnp.where(allowed[None], score, jnp.float32(-1e30))
        return (score, allowed, key3, value3)

    running = jnp.full((head_count, tok_rows), -1e30, jnp.float32)
    score, allowed, key3, value3 = scores(
        lax.all_gather(kv_pair, "ctx", axis=0, tiled=True), jnp.int32(0)
    )
    newest = jnp.maximum(running, jnp.max(score, axis=-1))
    expo = jnp.where(allowed[None], jnp.exp(score - newest[..., None]), jnp.float32(0.0))
    total = jnp.sum(expo, axis=-1)
    accum = jnp.einsum(
        "hsn,nhd->hsd", expo.astype(jnp.bfloat16), value3, preferred_element_type=jnp.float32
    )
    running, total, accum = (newest, total, accum)
    out_heads = (accum / total[..., None]).astype(jnp.bfloat16)
    lse = running + jnp.log(total)
    grad_heads = grad3.transpose(1, 0, 2)
    delta = jnp.sum(grad_heads.astype(jnp.float32) * out_heads.astype(jnp.float32), axis=-1)

    def grads_piece(piece, start):
        count = piece.shape[0]
        score, allowed, key3, value3 = scores(piece, start)
        prob = jnp.where(allowed[None], jnp.exp(score - lse[..., None]), jnp.float32(0.0))
        dprob = jnp.einsum("shd,nhd->hsn", grad3, value3, preferred_element_type=jnp.float32)
        dscore = (prob * (dprob - delta[..., None])).astype(jnp.bfloat16)
        dquery = (
            jnp.einsum("hsn,nhd->hsd", dscore, key3, preferred_element_type=jnp.float32) * scale
        )
        dkey = (
            jnp.einsum("hsn,shd->nhd", dscore, query3, preferred_element_type=jnp.float32) * scale
        )
        dvalue = jnp.einsum(
            "hsn,shd->nhd", prob.astype(jnp.bfloat16), grad3, preferred_element_type=jnp.float32
        )
        return (
            dquery,
            jnp.stack(
                [dkey.reshape(count, head_count * HS), dvalue.reshape(count, head_count * HS)],
                axis=1,
            ),
        )

    ctx_index = lax.axis_index("ctx")

    def turn(step, state):
        moving, gathered, dquery = state
        source = (ctx_index - step) % ctx_count
        dquery_add, term = grads_piece(moving, source * tok_rows)
        gathered = gathered + term
        dquery = dquery + dquery_add
        moving = shifted(moving, "ctx", 1)
        gathered = passed_along(gathered, "ctx", 1)
        return (moving, gathered, dquery)

    start_state = (
        kv_pair,
        jnp.zeros((tok_rows, 2, head_count * HS), jnp.float32),
        jnp.zeros((head_count, tok_rows, HS), jnp.float32),
    )
    moved, kv_grad, dquery = lax.fori_loop(0, ctx_count, turn, start_state)
    dkey_own = kv_grad[:, 0].reshape(tok_rows, head_count, HS)
    dvalue_own = kv_grad[:, 1].reshape(tok_rows, head_count, HS)
    dkey_full = jnp.einsum(
        "shd,hk->skd", dkey_own, chooser, precision=lax.Precision.HIGHEST
    ).reshape(tok_rows, kv_count * HS)
    dvalue_full = jnp.einsum(
        "shd,hk->skd", dvalue_own, chooser, precision=lax.Precision.HIGHEST
    ).reshape(tok_rows, kv_count * HS)
    d_keys, d_values = lax.psum((dkey_full, dvalue_full), "tp")
    attended = out_heads.transpose(1, 0, 2).reshape(tok_rows, head_count * HS)
    d_queries = dquery.transpose(1, 0, 2).reshape(tok_rows, head_count * HS).astype(jnp.bfloat16)
    return (attended, d_queries, d_keys.astype(jnp.bfloat16), d_values.astype(jnp.bfloat16))


def solution(mesh):
    return jax.shard_map(
        on_device,
        mesh=mesh,
        in_specs=(
            P("ctx", "tp"),
            P("ctx", None),
            P("ctx", None),
            P("ctx"),
            P("tp", None, None),
            P(),
            P("ctx", "tp"),
        ),
        out_specs=(P("ctx", "tp"), P("ctx", "tp"), P("ctx", None), P("ctx", None)),
        check_vma=False,
    )
```

profile of v0, /device:TPU:4, one launch (start us, length us, event | category | flops | bytes accessed | tf_op | source)
XLA Modules:
  0.0 874.1 jit_solution(2036602458892184687)
XLA Ops:
  10.7 71.9 %all-gather = s32[32,1,128]{2,1,0:T(1,128)S(1)} all-gather(s32[1,1,128]{2,1,0:T(1,128)} %bitcast.154), channel_id=1, replica_groups=mesh['ctx'=32,'tp'=24] {'ctx'}, dimensions={0}, use_global_device_ids=true | all-gather | bytes 16896 | tf_op jit(solution)/shard_map/all_gather | solution.py:39
  85.1 42.2 %all-gather.3.cloned.1.call-done = bf16[4096,2,128]{2,0,1:T(8,128)(2,1)} async-done(((bf16[128,2,128]{2,0,1:T(8,128)(2,1)}), bf16[4096,2,128]{2,0,1:T(8,128)(2,1)}) %all-gather.3.cloned.1.call-update) | async-done | bytes 2097168 | tf_op jit(solution)/shard_map/all_gather | solution.py:78
  132.8 582.8 %while.22 = (s32[]{:T(128)}, bf16[128,2,128]{2,0,1:T(8,128)(2,1)S(1)}, f32[128,2,128]{0,2,1:T(8,128)S(1)}, f32[1,128,128]{1,2,0:T(8,128)S(1)}, s32[]{:T(128)}, /...) while((s32[]{:T(128)}, ...), condition=%wide.region_4.5_spmd.clone.clone.clone, body=%wide.region_3.4_spmd.clone.clone.clone.sunk | while | flops 30779408 | bytes 2292666 | solution.py:132
  132.9 2.1 collective-permute-start
  136.4 2.4 collective-permute-start.1
  139.0 13.3 %collective-permute-done.1 = f32[128,2,128]{0,2,1:T(8,128)S(1)} collective-permute-done((f32[128,2,128]{0,2,1:T(8,128)S(1)}, f32[128,2,128]{0,2,1:T(8,128)S(1)}, u32[]{:S(2)}, u32[]{:S(2)}) %collective-permute-start.1) | collective-permute-done | bytes 131104 | tf_op jit(solution)/shard_map/while/body/eval_jaxpr/ppermute | solution.py:22
  155.1 1.9 collective-permute-start.1
  157.3 13.4 %collective-permute-done.1 = f32[128,2,128]{0,2,1:T(8,128)S(1)} collective-permute-done((f32[128,2,128]{0,2,1:T(8,128)S(1)}, f32[128,2,128]{0,2,1:T(8,128)S(1)}, u32[]{:S(2)}, u32[]{:S(2)}) %collective-permute-start.1) | collective-permute-done | bytes 131104 | tf_op jit(solution)/shard_map/while/body/eval_jaxpr/ppermute | solution.py:22
  173.4 1.9 collective-permute-start.1
  175.6 13.4 %collective-permute-done.1 = f32[128,2,128]{0,2,1:T(8,128)S(1)} collective-permute-done((f32[128,2,128]{0,2,1:T(8,128)S(1)}, f32[128,2,128]{0,2,1:T(8,128)S(1)}, u32[]{:S(2)}, u32[]{:S(2)}) %collective-permute-start.1) | collective-permute-done | bytes 131104 | tf_op jit(solution)/shard_map/while/body/eval_jaxpr/ppermute | solution.py:22
  191.7 1.9 collective-permute-start.1
  193.8 13.6 %collective-permute-done.1 = f32[128,2,128]{0,2,1:T(8,128)S(1)} collective-permute-done((f32[128,2,128]{0,2,1:T(8,128)S(1)}, f32[128,2,128]{0,2,1:T(8,128)S(1)}, u32[]{:S(2)}, u32[]{:S(2)}) %collective-permute-start.1) | collective-permute-done | bytes 131104 | tf_op jit(solution)/shard_map/while/body/eval_jaxpr/ppermute | solution.py:22
  210.1 1.9 collective-permute-start.1
  212.3 13.4 %collective-permute-done.1 = f32[128,2,128]{0,2,1:T(8,128)S(1)} collective-permute-done((f32[128,2,128]{0,2,1:T(8,128)S(1)}, f32[128,2,128]{0,2,1:T(8,128)S(1)}, u32[]{:S(2)}, u32[]{:S(2)}) %collective-permute-start.1) | collective-permute-done | bytes 131104 | tf_op jit(solution)/shard_map/while/body/eval_jaxpr/ppermute | solution.py:22
  228.4 1.9 collective-permute-start.1
  230.6 12.6 %collective-permute-done.1 = f32[128,2,128]{0,2,1:T(8,128)S(1)} collective-permute-done((f32[128,2,128]{0,2,1:T(8,128)S(1)}, f32[128,2,128]{0,2,1:T(8,128)S(1)}, u32[]{:S(2)}, u32[]{:S(2)}) %collective-permute-start.1) | collective-permute-done | bytes 131104 | tf_op jit(solution)/shard_map/while/body/eval_jaxpr/ppermute | solution.py:22
  245.9 1.9 collective-permute-start.1
  248.1 12.5 %collective-permute-done.1 = f32[128,2,128]{0,2,1:T(8,128)S(1)} collective-permute-done((f32[128,2,128]{0,2,1:T(8,128)S(1)}, f32[128,2,128]{0,2,1:T(8,128)S(1)}, u32[]{:S(2)}, u32[]{:S(2)}) %collective-permute-start.1) | collective-permute-done | bytes 131104 | tf_op jit(solution)/shard_map/while/body/eval_jaxpr/ppermute | solution.py:22
  263.3 1.9 collective-permute-start.1
  265.5 13.2 %collective-permute-done.1 = f32[128,2,128]{0,2,1:T(8,128)S(1)} collective-permute-done((f32[128,2,128]{0,2,1:T(8,128)S(1)}, f32[128,2,128]{0,2,1:T(8,128)S(1)}, u32[]{:S(2)}, u32[]{:S(2)}) %collective-permute-start.1) | collective-permute-done | bytes 131104 | tf_op jit(solution)/shard_map/while/body/eval_jaxpr/ppermute | solution.py:22
  281.4 1.9 collective-permute-start.1
  283.6 13.5 %collective-permute-done.1 = f32[128,2,128]{0,2,1:T(8,128)S(1)} collective-permute-done((f32[128,2,128]{0,2,1:T(8,128)S(1)}, f32[128,2,128]{0,2,1:T(8,128)S(1)}, u32[]{:S(2)}, u32[]{:S(2)}) %collective-permute-start.1) | collective-permute-done | bytes 131104 | tf_op jit(solution)/shard_map/while/body/eval_jaxpr/ppermute | solution.py:22
  299.8 1.9 collective-permute-start.1
  301.9 14.0 %collective-permute-done.1 = f32[128,2,128]{0,2,1:T(8,128)S(1)} collective-permute-done((f32[128,2,128]{0,2,1:T(8,128)S(1)}, f32[128,2,128]{0,2,1:T(8,128)S(1)}, u32[]{:S(2)}, u32[]{:S(2)}) %collective-permute-start.1) | collective-permute-done | bytes 131104 | tf_op jit(solution)/shard_map/while/body/eval_jaxpr/ppermute | solution.py:22
  318.6 1.9 collective-permute-start.1
  320.8 13.3 %collective-permute-done.1 = f32[128,2,128]{0,2,1:T(8,128)S(1)} collective-permute-done((f32[128,2,128]{0,2,1:T(8,128)S(1)}, f32[128,2,128]{0,2,1:T(8,128)S(1)}, u32[]{:S(2)}, u32[]{:S(2)}) %collective-permute-start.1) | collective-permute-done | bytes 131104 | tf_op jit(solution)/shard_map/while/body/eval_jaxpr/ppermute | solution.py:22
  336.9 1.9 collective-permute-start.1
  339.0 13.3 %collective-permute-done.1 = f32[128,2,128]{0,2,1:T(8,128)S(1)} collective-permute-done((f32[128,2,128]{0,2,1:T(8,128)S(1)}, f32[128,2,128]{0,2,1:T(8,128)S(1)}, u32[]{:S(2)}, u32[]{:S(2)}) %collective-permute-start.1) | collective-permute-done | bytes 131104 | tf_op jit(solution)/shard_map/while/body/eval_jaxpr/ppermute | solution.py:22
  355.0 1.9 collective-permute-start.1
  357.2 13.3 %collective-permute-done.1 = f32[128,2,128]{0,2,1:T(8,128)S(1)} collective-permute-done((f32[128,2,128]{0,2,1:T(8,128)S(1)}, f32[128,2,128]{0,2,1:T(8,128)S(1)}, u32[]{:S(2)}, u32[]{:S(2)}) %collective-permute-start.1) | collective-permute-done | bytes 131104 | tf_op jit(solution)/shard_map/while/body/eval_jaxpr/ppermute | solution.py:22
  373.1 1.9 collective-permute-start.1
  375.3 13.3 %collective-permute-done.1 = f32[128,2,128]{0,2,1:T(8,128)S(1)} collective-permute-done((f32[128,2,128]{0,2,1:T(8,128)S(1)}, f32[128,2,128]{0,2,1:T(8,128)S(1)}, u32[]{:S(2)}, u32[]{:S(2)}) %collective-permute-start.1) | collective-permute-done | bytes 131104 | tf_op jit(solution)/shard_map/while/body/eval_jaxpr/ppermute | solution.py:22
  391.3 1.9 collective-permute-start.1
  393.5 13.3 %collective-permute-done.1 = f32[128,2,128]{0,2,1:T(8,128)S(1)} collective-permute-done((f32[128,2,128]{0,2,1:T(8,128)S(1)}, f32[128,2,128]{0,2,1:T(8,128)S(1)}, u32[]{:S(2)}, u32[]{:S(2)}) %collective-permute-start.1) | collective-permute-done | bytes 131104 | tf_op jit(solution)/shard_map/while/body/eval_jaxpr/ppermute | solution.py:22
  409.4 1.9 collective-permute-start.1
  411.6 13.3 %collective-permute-done.1 = f32[128,2,128]{0,2,1:T(8,128)S(1)} collective-permute-done((f32[128,2,128]{0,2,1:T(8,128)S(1)}, f32[128,2,128]{0,2,1:T(8,128)S(1)}, u32[]{:S(2)}, u32[]{:S(2)}) %collective-permute-start.1) | collective-permute-done | bytes 131104 | tf_op jit(solution)/shard_map/while/body/eval_jaxpr/ppermute | solution.py:22
  427.6 1.9 collective-permute-start.1
  429.8 13.2 %collective-permute-done.1 = f32[128,2,128]{0,2,1:T(8,128)S(1)} collective-permute-done((f32[128,2,128]{0,2,1:T(8,128)S(1)}, f32[128,2,128]{0,2,1:T(8,128)S(1)}, u32[]{:S(2)}, u32[]{:S(2)}) %collective-permute-start.1) | collective-permute-done | bytes 131104 | tf_op jit(solution)/shard_map/while/body/eval_jaxpr/ppermute | solution.py:22
  445.6 1.9 collective-permute-start.1
  447.8 13.2 %collective-permute-done.1 = f32[128,2,128]{0,2,1:T(8,128)S(1)} collective-permute-done((f32[128,2,128]{0,2,1:T(8,128)S(1)}, f32[128,2,128]{0,2,1:T(8,128)S(1)}, u32[]{:S(2)}, u32[]{:S(2)}) %collective-permute-start.1) | collective-permute-done | bytes 131104 | tf_op jit(solution)/shard_map/while/body/eval_jaxpr/ppermute | solution.py:22
  463.7 1.9 collective-permute-start.1
  465.8 13.2 %collective-permute-done.1 = f32[128,2,128]{0,2,1:T(8,128)S(1)} collective-permute-done((f32[128,2,128]{0,2,1:T(8,128)S(1)}, f32[128,2,128]{0,2,1:T(8,128)S(1)}, u32[]{:S(2)}, u32[]{:S(2)}) %collective-permute-start.1) | collective-permute-done | bytes 131104 | tf_op jit(solution)/shard_map/while/body/eval_jaxpr/ppermute | solution.py:22
  481.7 1.9 collective-permute-start.1
  483.9 13.2 %collective-permute-done.1 = f32[128,2,128]{0,2,1:T(8,128)S(1)} collective-permute-done((f32[128,2,128]{0,2,1:T(8,128)S(1)}, f32[128,2,128]{0,2,1:T(8,128)S(1)}, u32[]{:S(2)}, u32[]{:S(2)}) %collective-permute-start.1) | collective-permute-done | bytes 131104 | tf_op jit(solution)/shard_map/while/body/eval_jaxpr/ppermute | solution.py:22
  499.7 1.9 collective-permute-start.1
  501.9 13.2 %collective-permute-done.1 = f32[128,2,128]{0,2,1:T(8,128)S(1)} collective-permute-done((f32[128,2,128]{0,2,1:T(8,128)S(1)}, f32[128,2,128]{0,2,1:T(8,128)S(1)}, u32[]{:S(2)}, u32[]{:S(2)}) %collective-permute-start.1) | collective-permute-done | bytes 131104 | tf_op jit(solution)/shard_map/while/body/eval_jaxpr/ppermute | solution.py:22
  517.9 1.9 collective-permute-start.1
  520.1 13.3 %collective-permute-done.1 = f32[128,2,128]{0,2,1:T(8,128)S(1)} collective-permute-done((f32[128,2,128]{0,2,1:T(8,128)S(1)}, f32[128,2,128]{0,2,1:T(8,128)S(1)}, u32[]{:S(2)}, u32[]{:S(2)}) %collective-permute-start.1) | collective-permute-done | bytes 131104 | tf_op jit(solution)/shard_map/while/body/eval_jaxpr/ppermute | solution.py:22
  536.1 1.9 collective-permute-start.1
  538.3 13.3 %collective-permute-done.1 = f32[128,2,128]{0,2,1:T(8,128)S(1)} collective-permute-done((f32[128,2,128]{0,2,1:T(8,128)S(1)}, f32[128,2,128]{0,2,1:T(8,128)S(1)}, u32[]{:S(2)}, u32[]{:S(2)}) %collective-permute-start.1) | collective-permute-done | bytes 131104 | tf_op jit(solution)/shard_map/while/body/eval_jaxpr/ppermute | solution.py:22
  554.3 1.9 collective-permute-start.1
  556.5 13.3 %collective-permute-done.1 = f32[128,2,128]{0,2,1:T(8,128)S(1)} collective-permute-done((f32[128,2,128]{0,2,1:T(8,128)S(1)}, f32[128,2,128]{0,2,1:T(8,128)S(1)}, u32[]{:S(2)}, u32[]{:S(2)}) %collective-permute-start.1) | collective-permute-done | bytes 131104 | tf_op jit(solution)/shard_map/while/body/eval_jaxpr/ppermute | solution.py:22
  574.7 13.3 %collective-permute-done.1 = f32[128,2,128]{0,2,1:T(8,128)S(1)} collective-permute-done((f32[128,2,128]{0,2,1:T(8,128)S(1)}, f32[128,2,128]{0,2,1:T(8,128)S(1)}, u32[]{:S(2)}, u32[]{:S(2)}) %collective-permute-start.1) | collective-permute-done | bytes 131104 | tf_op jit(solution)/shard_map/while/body/eval_jaxpr/ppermute | solution.py:22
  593.0 13.3 %collective-permute-done.1 = f32[128,2,128]{0,2,1:T(8,128)S(1)} collective-permute-done((f32[128,2,128]{0,2,1:T(8,128)S(1)}, f32[128,2,128]{0,2,1:T(8,128)S(1)}, u32[]{:S(2)}, u32[]{:S(2)}) %collective-permute-start.1) | collective-permute-done | bytes 131104 | tf_op jit(solution)/shard_map/while/body/eval_jaxpr/ppermute | solution.py:22
  609.0 1.9 collective-permute-start.1
  611.2 13.3 %collective-permute-done.1 = f32[128,2,128]{0,2,1:T(8,128)S(1)} collective-permute-done((f32[128,2,128]{0,2,1:T(8,128)S(1)}, f32[128,2,128]{0,2,1:T(8,128)S(1)}, u32[]{:S(2)}, u32[]{:S(2)}) %collective-permute-start.1) | collective-permute-done | bytes 131104 | tf_op jit(solution)/shard_map/while/body/eval_jaxpr/ppermute | solution.py:22
  629.4 13.3 %collective-permute-done.1 = f32[128,2,128]{0,2,1:T(8,128)S(1)} collective-permute-done((f32[128,2,128]{0,2,1:T(8,128)S(1)}, f32[128,2,128]{0,2,1:T(8,128)S(1)}, u32[]{:S(2)}, u32[]{:S(2)}) %collective-permute-start.1) | collective-permute-done | bytes 131104 | tf_op jit(solution)/shard_map/while/body/eval_jaxpr/ppermute | solution.py:22
  647.6 13.3 %collective-permute-done.1 = f32[128,2,128]{0,2,1:T(8,128)S(1)} collective-permute-done((f32[128,2,128]{0,2,1:T(8,128)S(1)}, f32[128,2,128]{0,2,1:T(8,128)S(1)}, u32[]{:S(2)}, u32[]{:S(2)}) %collective-permute-start.1) | collective-permute-done | bytes 131104 | tf_op jit(solution)/shard_map/while/body/eval_jaxpr/ppermute | solution.py:22
  663.7 1.9 collective-permute-start.1
  665.9 13.3 %collective-permute-done.1 = f32[128,2,128]{0,2,1:T(8,128)S(1)} collective-permute-done((f32[128,2,128]{0,2,1:T(8,128)S(1)}, f32[128,2,128]{0,2,1:T(8,128)S(1)}, u32[]{:S(2)}, u32[]{:S(2)}) %collective-permute-start.1) | collective-permute-done | bytes 131104 | tf_op jit(solution)/shard_map/while/body/eval_jaxpr/ppermute | solution.py:22
  684.1 13.3 %collective-permute-done.1 = f32[128,2,128]{0,2,1:T(8,128)S(1)} collective-permute-done((f32[128,2,128]{0,2,1:T(8,128)S(1)}, f32[128,2,128]{0,2,1:T(8,128)S(1)}, u32[]{:S(2)}, u32[]{:S(2)}) %collective-permute-start.1) | collective-permute-done | bytes 131104 | tf_op jit(solution)/shard_map/while/body/eval_jaxpr/ppermute | solution.py:22
  700.1 1.9 collective-permute-start.1
  702.3 13.3 %collective-permute-done.1 = f32[128,2,128]{0,2,1:T(8,128)S(1)} collective-permute-done((f32[128,2,128]{0,2,1:T(8,128)S(1)}, f32[128,2,128]{0,2,1:T(8,128)S(1)}, u32[]{:S(2)}, u32[]{:S(2)}) %collective-permute-start.1) | collective-permute-done | bytes 131104 | tf_op jit(solution)/shard_map/while/body/eval_jaxpr/ppermute | solution.py:22
  715.8 148.4 %all-reduce.2 = (bf16[128,768]{0,1:T(8,128)(2,1)S(1)}, bf16[128,768]{0,1:T(8,128)(2,1)S(1)}) all-reduce(f32[128,768]{0,1:T(8,128)S(1)} %bitcast.146, f32[128,768]{0,1:T(8,128)S(1)} %bitcast.145), channel_id=1, replica_groups=mesh['ctx'=32,'tp'=24] {'tp'}, use_global_device_ids=true, to_apply=%region_5.6 | all-reduce | flops 196608 | bytes 1179648 | tf_op jit(solution)/shard_map/psum | solution.py:141
  (488 shorter events, 114.1 us)
Async XLA Ops:
  7.2 120.1 %all-gather.3.cloned.1.call-start = ((), (), s32[]{:S(2)}) async-start(), calls=%async_computation | async-start | bytes 2162688 | tf_op jit(solution)/shard_map/all_gather | solution.py:78
  132.9 6.2 collective-permute-start
  136.4 16.0 %collective-permute-start.1 = (f32[128,2,128]{0,2,1:T(8,128)S(1)}, f32[128,2,128]{0,2,1:T(8,128)S(1)}, u32[]{:S(2)}, u32[]{:S(2)}) collective-permute-start(f32[128,2,128]{0,2,1:T(8,128)S(1)} %maximum_add_fusion.2), channel_id=1, source_target_pairs={{0,24},{24,48},{48,72},{72,96},{96,120},{120,144},{144,168},{168,1... | collective-permute-start | bytes 393224 | tf_op jit(solution)/shard_map/while/body/eval_jaxpr/ppermute | solution.py:22
  152.4 4.9 collective-permute-start
  155.1 15.6 %collective-permute-start.1 = (f32[128,2,128]{0,2,1:T(8,128)S(1)}, f32[128,2,128]{0,2,1:T(8,128)S(1)}, u32[]{:S(2)}, u32[]{:S(2)}) collective-permute-start(f32[128,2,128]{0,2,1:T(8,128)S(1)} %maximum_add_fusion.2), channel_id=1, source_target_pairs={{0,24},{24,48},{48,72},{72,96},{96,120},{120,144},{144,168},{168,1... | collective-permute-start | bytes 393224 | tf_op jit(solution)/shard_map/while/body/eval_jaxpr/ppermute | solution.py:22
  170.7 4.9 collective-permute-start
  173.4 15.6 %collective-permute-start.1 = (f32[128,2,128]{0,2,1:T(8,128)S(1)}, f32[128,2,128]{0,2,1:T(8,128)S(1)}, u32[]{:S(2)}, u32[]{:S(2)}) collective-permute-start(f32[128,2,128]{0,2,1:T(8,128)S(1)} %maximum_add_fusion.2), channel_id=1, source_target_pairs={{0,24},{24,48},{48,72},{72,96},{96,120},{120,144},{144,168},{168,1... | collective-permute-start | bytes 393224 | tf_op jit(solution)/shard_map/while/body/eval_jaxpr/ppermute | solution.py:22
  189.0 4.9 collective-permute-start
  191.7 15.7 %collective-permute-start.1 = (f32[128,2,128]{0,2,1:T(8,128)S(1)}, f32[128,2,128]{0,2,1:T(8,128)S(1)}, u32[]{:S(2)}, u32[]{:S(2)}) collective-permute-start(f32[128,2,128]{0,2,1:T(8,128)S(1)} %maximum_add_fusion.2), channel_id=1, source_target_pairs={{0,24},{24,48},{48,72},{72,96},{96,120},{120,144},{144,168},{168,1... | collective-permute-start | bytes 393224 | tf_op jit(solution)/shard_map/while/body/eval_jaxpr/ppermute | solution.py:22
  207.4 4.9 collective-permute-start
  210.1 15.6 %collective-permute-start.1 = (f32[128,2,128]{0,2,1:T(8,128)S(1)}, f32[128,2,128]{0,2,1:T(8,128)S(1)}, u32[]{:S(2)}, u32[]{:S(2)}) collective-permute-start(f32[128,2,128]{0,2,1:T(8,128)S(1)} %maximum_add_fusion.2), channel_id=1, source_target_pairs={{0,24},{24,48},{48,72},{72,96},{96,120},{120,144},{144,168},{168,1... | collective-permute-start | bytes 393224 | tf_op jit(solution)/shard_map/while/body/eval_jaxpr/ppermute | solution.py:22
  225.7 4.9 collective-permute-start
  228.4 14.8 %collective-permute-start.1 = (f32[128,2,128]{0,2,1:T(8,128)S(1)}, f32[128,2,128]{0,2,1:T(8,128)S(1)}, u32[]{:S(2)}, u32[]{:S(2)}) collective-permute-start(f32[128,2,128]{0,2,1:T(8,128)S(1)} %maximum_add_fusion.2), channel_id=1, source_target_pairs={{0,24},{24,48},{48,72},{72,96},{96,120},{120,144},{144,168},{168,1... | collective-permute-start | bytes 393224 | tf_op jit(solution)/shard_map/while/body/eval_jaxpr/ppermute | solution.py:22
  243.2 4.9 collective-permute-start
  245.9 14.7 %collective-permute-start.1 = (f32[128,2,128]{0,2,1:T(8,128)S(1)}, f32[128,2,128]{0,2,1:T(8,128)S(1)}, u32[]{:S(2)}, u32[]{:S(2)}) collective-permute-start(f32[128,2,128]{0,2,1:T(8,128)S(1)} %maximum_add_fusion.2), channel_id=1, source_target_pairs={{0,24},{24,48},{48,72},{72,96},{96,120},{120,144},{144,168},{168,1... | collective-permute-start | bytes 393224 | tf_op jit(solution)/shard_map/while/body/eval_jaxpr/ppermute | solution.py:22
  260.6 4.9 collective-permute-start
  263.3 15.4 %collective-permute-start.1 = (f32[128,2,128]{0,2,1:T(8,128)S(1)}, f32[128,2,128]{0,2,1:T(8,128)S(1)}, u32[]{:S(2)}, u32[]{:S(2)}) collective-permute-start(f32[128,2,128]{0,2,1:T(8,128)S(1)} %maximum_add_fusion.2), channel_id=1, source_target_pairs={{0,24},{24,48},{48,72},{72,96},{96,120},{120,144},{144,168},{168,1... | collective-permute-start | bytes 393224 | tf_op jit(solution)/shard_map/while/body/eval_jaxpr/ppermute | solution.py:22
  278.7 4.9 collective-permute-start
  281.4 15.6 %collective-permute-start.1 = (f32[128,2,128]{0,2,1:T(8,128)S(1)}, f32[128,2,128]{0,2,1:T(8,128)S(1)}, u32[]{:S(2)}, u32[]{:S(2)}) collective-permute-start(f32[128,2,128]{0,2,1:T(8,128)S(1)} %maximum_add_fusion.2), channel_id=1, source_target_pairs={{0,24},{24,48},{48,72},{72,96},{96,120},{120,144},{144,168},{168,1... | collective-permute-start | bytes 393224 | tf_op jit(solution)/shard_map/while/body/eval_jaxpr/ppermute | solution.py:22
  297.1 4.9 collective-permute-start
  299.8 16.2 %collective-permute-start.1 = (f32[128,2,128]{0,2,1:T(8,128)S(1)}, f32[128,2,128]{0,2,1:T(8,128)S(1)}, u32[]{:S(2)}, u32[]{:S(2)}) collective-permute-start(f32[128,2,128]{0,2,1:T(8,128)S(1)} %maximum_add_fusion.2), channel_id=1, source_target_pairs={{0,24},{24,48},{48,72},{72,96},{96,120},{120,144},{144,168},{168,1... | collective-permute-start | bytes 393224 | tf_op jit(solution)/shard_map/while/body/eval_jaxpr/ppermute | solution.py:22
  315.9 4.9 collective-permute-start
  318.6 15.5 %collective-permute-start.1 = (f32[128,2,128]{0,2,1:T(8,128)S(1)}, f32[128,2,128]{0,2,1:T(8,128)S(1)}, u32[]{:S(2)}, u32[]{:S(2)}) collective-permute-start(f32[128,2,128]{0,2,1:T(8,128)S(1)} %maximum_add_fusion.2), channel_id=1, source_target_pairs={{0,24},{24,48},{48,72},{72,96},{96,120},{120,144},{144,168},{168,1... | collective-permute-start | bytes 393224 | tf_op jit(solution)/shard_map/while/body/eval_jaxpr/ppermute | solution.py:22
  334.2 4.9 collective-permute-start
  336.9 15.4 %collective-permute-start.1 = (f32[128,2,128]{0,2,1:T(8,128)S(1)}, f32[128,2,128]{0,2,1:T(8,128)S(1)}, u32[]{:S(2)}, u32[]{:S(2)}) collective-permute-start(f32[128,2,128]{0,2,1:T(8,128)S(1)} %maximum_add_fusion.2), channel_id=1, source_target_pairs={{0,24},{24,48},{48,72},{72,96},{96,120},{120,144},{144,168},{168,1... | collective-permute-start | bytes 393224 | tf_op jit(solution)/shard_map/while/body/eval_jaxpr/ppermute | solution.py:22
  352.3 4.9 collective-permute-start
  355.0 15.4 %collective-permute-start.1 = (f32[128,2,128]{0,2,1:T(8,128)S(1)}, f32[128,2,128]{0,2,1:T(8,128)S(1)}, u32[]{:S(2)}, u32[]{:S(2)}) collective-permute-start(f32[128,2,128]{0,2,1:T(8,128)S(1)} %maximum_add_fusion.2), channel_id=1, source_target_pairs={{0,24},{24,48},{48,72},{72,96},{96,120},{120,144},{144,168},{168,1... | collective-permute-start | bytes 393224 | tf_op jit(solution)/shard_map/while/body/eval_jaxpr/ppermute | solution.py:22
  370.4 4.9 collective-permute-start
  373.1 15.4 %collective-permute-start.1 = (f32[128,2,128]{0,2,1:T(8,128)S(1)}, f32[128,2,128]{0,2,1:T(8,128)S(1)}, u32[]{:S(2)}, u32[]{:S(2)}) collective-permute-start(f32[128,2,128]{0,2,1:T(8,128)S(1)} %maximum_add_fusion.2), channel_id=1, source_target_pairs={{0,24},{24,48},{48,72},{72,96},{96,120},{120,144},{144,168},{168,1... | collective-permute-start | bytes 393224 | tf_op jit(solution)/shard_map/while/body/eval_jaxpr/ppermute | solution.py:22
  388.6 4.9 collective-permute-start
  391.3 15.4 %collective-permute-start.1 = (f32[128,2,128]{0,2,1:T(8,128)S(1)}, f32[128,2,128]{0,2,1:T(8,128)S(1)}, u32[]{:S(2)}, u32[]{:S(2)}) collective-permute-start(f32[128,2,128]{0,2,1:T(8,128)S(1)} %maximum_add_fusion.2), channel_id=1, source_target_pairs={{0,24},{24,48},{48,72},{72,96},{96,120},{120,144},{144,168},{168,1... | collective-permute-start | bytes 393224 | tf_op jit(solution)/shard_map/while/body/eval_jaxpr/ppermute | solution.py:22
  406.7 4.9 collective-permute-start
  409.4 15.4 %collective-permute-start.1 = (f32[128,2,128]{0,2,1:T(8,128)S(1)}, f32[128,2,128]{0,2,1:T(8,128)S(1)}, u32[]{:S(2)}, u32[]{:S(2)}) collective-permute-start(f32[128,2,128]{0,2,1:T(8,128)S(1)} %maximum_add_fusion.2), channel_id=1, source_target_pairs={{0,24},{24,48},{48,72},{72,96},{96,120},{120,144},{144,168},{168,1... | collective-permute-start | bytes 393224 | tf_op jit(solution)/shard_map/while/body/eval_jaxpr/ppermute | solution.py:22
  424.9 4.9 collective-permute-start
  427.6 15.3 %collective-permute-start.1 = (f32[128,2,128]{0,2,1:T(8,128)S(1)}, f32[128,2,128]{0,2,1:T(8,128)S(1)}, u32[]{:S(2)}, u32[]{:S(2)}) collective-permute-start(f32[128,2,128]{0,2,1:T(8,128)S(1)} %maximum_add_fusion.2), channel_id=1, source_target_pairs={{0,24},{24,48},{48,72},{72,96},{96,120},{120,144},{144,168},{168,1... | collective-permute-start | bytes 393224 | tf_op jit(solution)/shard_map/while/body/eval_jaxpr/ppermute | solution.py:22
  442.9 4.9 collective-permute-start
  445.6 15.3 %collective-permute-start.1 = (f32[128,2,128]{0,2,1:T(8,128)S(1)}, f32[128,2,128]{0,2,1:T(8,128)S(1)}, u32[]{:S(2)}, u32[]{:S(2)}) collective-permute-start(f32[128,2,128]{0,2,1:T(8,128)S(1)} %maximum_add_fusion.2), channel_id=1, source_target_pairs={{0,24},{24,48},{48,72},{72,96},{96,120},{120,144},{144,168},{168,1... | collective-permute-start | bytes 393224 | tf_op jit(solution)/shard_map/while/body/eval_jaxpr/ppermute | solution.py:22
  461.0 4.9 collective-permute-start
  463.7 15.3 %collective-permute-start.1 = (f32[128,2,128]{0,2,1:T(8,128)S(1)}, f32[128,2,128]{0,2,1:T(8,128)S(1)}, u32[]{:S(2)}, u32[]{:S(2)}) collective-permute-start(f32[128,2,128]{0,2,1:T(8,128)S(1)} %maximum_add_fusion.2), channel_id=1, source_target_pairs={{0,24},{24,48},{48,72},{72,96},{96,120},{120,144},{144,168},{168,1... | collective-permute-start | bytes 393224 | tf_op jit(solution)/shard_map/while/body/eval_jaxpr/ppermute | solution.py:22
  479.0 4.9 collective-permute-start
  481.7 15.3 %collective-permute-start.1 = (f32[128,2,128]{0,2,1:T(8,128)S(1)}, f32[128,2,128]{0,2,1:T(8,128)S(1)}, u32[]{:S(2)}, u32[]{:S(2)}) collective-permute-start(f32[128,2,128]{0,2,1:T(8,128)S(1)} %maximum_add_fusion.2), channel_id=1, source_target_pairs={{0,24},{24,48},{48,72},{72,96},{96,120},{120,144},{144,168},{168,1... | collective-permute-start | bytes 393224 | tf_op jit(solution)/shard_map/while/body/eval_jaxpr/ppermute | solution.py:22
  497.0 4.9 collective-permute-start
  499.7 15.4 %collective-permute-start.1 = (f32[128,2,128]{0,2,1:T(8,128)S(1)}, f32[128,2,128]{0,2,1:T(8,128)S(1)}, u32[]{:S(2)}, u32[]{:S(2)}) collective-permute-start(f32[128,2,128]{0,2,1:T(8,128)S(1)} %maximum_add_fusion.2), channel_id=1, source_target_pairs={{0,24},{24,48},{48,72},{72,96},{96,120},{120,144},{144,168},{168,1... | collective-permute-start | bytes 393224 | tf_op jit(solution)/shard_map/while/body/eval_jaxpr/ppermute | solution.py:22
  515.2 4.9 collective-permute-start
  517.9 15.5 %collective-permute-start.1 = (f32[128,2,128]{0,2,1:T(8,128)S(1)}, f32[128,2,128]{0,2,1:T(8,128)S(1)}, u32[]{:S(2)}, u32[]{:S(2)}) collective-permute-start(f32[128,2,128]{0,2,1:T(8,128)S(1)} %maximum_add_fusion.2), channel_id=1, source_target_pairs={{0,24},{24,48},{48,72},{72,96},{96,120},{120,144},{144,168},{168,1... | collective-permute-start | bytes 393224 | tf_op jit(solution)/shard_map/while/body/eval_jaxpr/ppermute | solution.py:22
  533.4 4.9 collective-permute-start
  536.1 15.5 %collective-permute-start.1 = (f32[128,2,128]{0,2,1:T(8,128)S(1)}, f32[128,2,128]{0,2,1:T(8,128)S(1)}, u32[]{:S(2)}, u32[]{:S(2)}) collective-permute-start(f32[128,2,128]{0,2,1:T(8,128)S(1)} %maximum_add_fusion.2), channel_id=1, source_target_pairs={{0,24},{24,48},{48,72},{72,96},{96,120},{120,144},{144,168},{168,1... | collective-permute-start | bytes 393224 | tf_op jit(solution)/shard_map/while/body/eval_jaxpr/ppermute | solution.py:22
  551.6 4.9 collective-permute-start
  554.3 15.5 %collective-permute-start.1 = (f32[128,2,128]{0,2,1:T(8,128)S(1)}, f32[128,2,128]{0,2,1:T(8,128)S(1)}, u32[]{:S(2)}, u32[]{:S(2)}) collective-permute-start(f32[128,2,128]{0,2,1:T(8,128)S(1)} %maximum_add_fusion.2), channel_id=1, source_target_pairs={{0,24},{24,48},{48,72},{72,96},{96,120},{120,144},{144,168},{168,1... | collective-permute-start | bytes 393224 | tf_op jit(solution)/shard_map/while/body/eval_jaxpr/ppermute | solution.py:22
  572.5 15.5 %collective-permute-start.1 = (f32[128,2,128]{0,2,1:T(8,128)S(1)}, f32[128,2,128]{0,2,1:T(8,128)S(1)}, u32[]{:S(2)}, u32[]{:S(2)}) collective-permute-start(f32[128,2,128]{0,2,1:T(8,128)S(1)} %maximum_add_fusion.2), channel_id=1, source_target_pairs={{0,24},{24,48},{48,72},{72,96},{96,120},{120,144},{144,168},{168,1... | collective-permute-start | bytes 393224 | tf_op jit(solution)/shard_map/while/body/eval_jaxpr/ppermute | solution.py:22
  588.1 4.9 collective-permute-start
  590.8 15.5 %collective-permute-start.1 = (f32[128,2,128]{0,2,1:T(8,128)S(1)}, f32[128,2,128]{0,2,1:T(8,128)S(1)}, u32[]{:S(2)}, u32[]{:S(2)}) collective-permute-start(f32[128,2,128]{0,2,1:T(8,128)S(1)} %maximum_add_fusion.2), channel_id=1, source_target_pairs={{0,24},{24,48},{48,72},{72,96},{96,120},{120,144},{144,168},{168,1... | collective-permute-start | bytes 393224 | tf_op jit(solution)/shard_map/while/body/eval_jaxpr/ppermute | solution.py:22
  606.3 4.9 collective-permute-start
  609.0 15.5 %collective-permute-start.1 = (f32[128,2,128]{0,2,1:T(8,128)S(1)}, f32[128,2,128]{0,2,1:T(8,128)S(1)}, u32[]{:S(2)}, u32[]{:S(2)}) collective-permute-start(f32[128,2,128]{0,2,1:T(8,128)S(1)} %maximum_add_fusion.2), channel_id=1, source_target_pairs={{0,24},{24,48},{48,72},{72,96},{96,120},{120,144},{144,168},{168,1... | collective-permute-start | bytes 393224 | tf_op jit(solution)/shard_map/while/body/eval_jaxpr/ppermute | solution.py:22
  624.5 4.9 collective-permute-start
  627.2 15.5 %collective-permute-start.1 = (f32[128,2,128]{0,2,1:T(8,128)S(1)}, f32[128,2,128]{0,2,1:T(8,128)S(1)}, u32[]{:S(2)}, u32[]{:S(2)}) collective-permute-start(f32[128,2,128]{0,2,1:T(8,128)S(1)} %maximum_add_fusion.2), channel_id=1, source_target_pairs={{0,24},{24,48},{48,72},{72,96},{96,120},{120,144},{144,168},{168,1... | collective-permute-start | bytes 393224 | tf_op jit(solution)/shard_map/while/body/eval_jaxpr/ppermute | solution.py:22
  642.8 4.9 collective-permute-start
  645.5 15.5 %collective-permute-start.1 = (f32[128,2,128]{0,2,1:T(8,128)S(1)}, f32[128,2,128]{0,2,1:T(8,128)S(1)}, u32[]{:S(2)}, u32[]{:S(2)}) collective-permute-start(f32[128,2,128]{0,2,1:T(8,128)S(1)} %maximum_add_fusion.2), channel_id=1, source_target_pairs={{0,24},{24,48},{48,72},{72,96},{96,120},{120,144},{144,168},{168,1... | collective-permute-start | bytes 393224 | tf_op jit(solution)/shard_map/while/body/eval_jaxpr/ppermute | solution.py:22
  661.0 4.9 collective-permute-start
  663.7 15.5 %collective-permute-start.1 = (f32[128,2,128]{0,2,1:T(8,128)S(1)}, f32[128,2,128]{0,2,1:T(8,128)S(1)}, u32[]{:S(2)}, u32[]{:S(2)}) collective-permute-start(f32[128,2,128]{0,2,1:T(8,128)S(1)} %maximum_add_fusion.2), channel_id=1, source_target_pairs={{0,24},{24,48},{48,72},{72,96},{96,120},{120,144},{144,168},{168,1... | collective-permute-start | bytes 393224 | tf_op jit(solution)/shard_map/while/body/eval_jaxpr/ppermute | solution.py:22
  679.2 4.9 collective-permute-start
  681.9 15.5 %collective-permute-start.1 = (f32[128,2,128]{0,2,1:T(8,128)S(1)}, f32[128,2,128]{0,2,1:T(8,128)S(1)}, u32[]{:S(2)}, u32[]{:S(2)}) collective-permute-start(f32[128,2,128]{0,2,1:T(8,128)S(1)} %maximum_add_fusion.2), channel_id=1, source_target_pairs={{0,24},{24,48},{48,72},{72,96},{96,120},{120,144},{144,168},{168,1... | collective-permute-start | bytes 393224 | tf_op jit(solution)/shard_map/while/body/eval_jaxpr/ppermute | solution.py:22
  697.4 4.9 collective-permute-start
  700.1 15.5 %collective-permute-start.1 = (f32[128,2,128]{0,2,1:T(8,128)S(1)}, f32[128,2,128]{0,2,1:T(8,128)S(1)}, u32[]{:S(2)}, u32[]{:S(2)}) collective-permute-start(f32[128,2,128]{0,2,1:T(8,128)S(1)} %maximum_add_fusion.2), channel_id=1, source_target_pairs={{0,24},{24,48},{48,72},{72,96},{96,120},{120,144},{144,168},{168,1... | collective-permute-start | bytes 393224 | tf_op jit(solution)/shard_map/while/body/eval_jaxpr/ppermute | solution.py:22
  (6 other events, 129.2 us)
Sparse Core Ops, SparseCore 0:
  12.5 114.7 all-gather.2
where the time goes:
time: 878 us; the launch traced here: 874 us
  waiting for transfers between devices  467 us (53%)
  blocking collectives  220 us (25%)
  starting transfers between devices  104 us (12%)
  matrix products  52.8 us (6%)
  between operations  14.2 us (2%)
  local copies, waits for them, and re-layouts  9.07 us (1%)
    ppermute x32, waiting for transfers between devices, passed_along(): return lax.ppermute(value, axis, pairs)  425 us
    psum x1, blocking collectives, on_device(): d_keys, d_values = lax.psum((dkey_full, dvalue_full), 'tp')  148 us
    all_gather x1, blocking collectives, on_device(): all_roles = lax.all_gather(roles, 'ctx', axis=0, tiled=True)  71.9 us
    ppermute x32, starting transfers between devices, passed_along(): return lax.ppermute(value, axis, pairs)  61.9 us
    all_gather x1, waiting for transfers between devices, on_device(): lax.all_gather(kv_pair, 'ctx', axis=0, tiled=True)  42.2 us
    ppermute x32, starting transfers between devices, shifted(): return lax.ppermute(block, axis, route)  41.9 us
  transfers between devices with their start and end apart: 65, of which 33 were waited for; matrix products, arithmetic and copies ran while one was open for 6% of the time, Pallas kernels for 0%

commit v1 on v0

v1 whole, which is shorter than its diff:
```python
import math

import jax
import jax.numpy as jnp
import numpy as np
from jax import lax
from jax.sharding import Mesh
from jax.sharding import PartitionSpec as P

HS = 128
GROUP = 4
BLK = 128
NEG = -1e30
HI = lax.Precision.HIGHEST


def on_device(queries, keys, values, roles, role_table, block_mask, d_out):
    rows = queries.shape[0]
    role_count = role_table.shape[1]
    scale = 1.0 / math.sqrt(HS)
    ctx_index = lax.axis_index("ctx")
    group = lax.axis_index("g")
    own_keys = lax.dynamic_slice_in_dim(keys, group * HS, HS, 1)
    own_values = lax.dynamic_slice_in_dim(values, group * HS, HS, 1)
    table = role_table[0]

    role_onehot = (roles[:, None] == jnp.arange(role_count)[None, :]).astype(jnp.float32)
    role_slot = jnp.pad(role_onehot, ((0, 0), (0, HS - role_count))).astype(jnp.bfloat16)
    packed = jnp.stack([own_keys, own_values, queries, d_out, role_slot], axis=1)
    every = lax.all_gather(packed, "ctx", axis=0, tiled=True)
    total_rows = every.shape[0]
    all_keys = every[:, 0]
    all_values = every[:, 1]
    all_queries = every[:, 2]
    all_grads = every[:, 3]
    all_onehot = every[:, 4, :role_count].astype(jnp.float32)

    pos = jnp.arange(total_rows)
    own_pos = ctx_index * rows + jnp.arange(rows)
    mask_f = block_mask.astype(jnp.float32)
    all_block = (pos[:, None] // BLK == jnp.arange(block_mask.shape[0])[None, :]).astype(jnp.float32)
    own_block = (own_pos[:, None] // BLK == jnp.arange(block_mask.shape[0])[None, :]).astype(jnp.float32)

    q_open = jnp.dot(jnp.dot(own_block, mask_f, precision=HI), all_block.T, precision=HI) > 0.5
    q_allowed = (pos[None, :] <= own_pos[:, None]) & (
        q_open | (pos[None, :] // BLK == own_pos[:, None] // BLK)
    )
    q_bias = jnp.dot(jnp.dot(role_onehot, table, precision=HI), all_onehot.T, precision=HI)
    score = jnp.dot(queries, all_keys.T, preferred_element_type=jnp.float32) * scale + q_bias
    score = jnp.where(q_allowed, score, jnp.float32(NEG))
    top = jnp.max(score, axis=-1)
    expo = jnp.where(q_allowed, jnp.exp(score - top[:, None]), jnp.float32(0.0))
    total = jnp.sum(expo, axis=-1)
    out = jnp.dot(expo.astype(jnp.bfloat16), all_values, preferred_element_type=jnp.float32)
    out = (out / total[:, None]).astype(jnp.bfloat16)
    lse = top + jnp.log(total)
    delta = jnp.sum(d_out.astype(jnp.float32) * out.astype(jnp.float32), axis=-1)
    prob = jnp.where(q_allowed, jnp.exp(score - lse[:, None]), jnp.float32(0.0))
    dprob = jnp.dot(d_out, all_values.T, preferred_element_type=jnp.float32)
    dscore = (prob * (dprob - delta[:, None])).astype(jnp.bfloat16)
    d_query = jnp.dot(dscore, all_keys, preferred_element_type=jnp.float32) * scale

    stats = lax.all_gather(jnp.stack([lse, delta], axis=0), "ctx", axis=1, tiled=True)
    all_lse = stats[0]
    all_delta = stats[1]

    k_open = jnp.dot(jnp.dot(all_block, mask_f, precision=HI), own_block.T, precision=HI) > 0.5
    k_allowed = (own_pos[None, :] <= pos[:, None]) & (
        k_open | (own_pos[None, :] // BLK == pos[:, None] // BLK)
    )
    k_bias = jnp.dot(all_onehot, jnp.dot(table, role_onehot.T, precision=HI), precision=HI)
    score_t = jnp.dot(all_queries, own_keys.T, preferred_element_type=jnp.float32) * scale + k_bias
    prob_t = jnp.where(k_allowed, jnp.exp(score_t - all_lse[:, None]), jnp.float32(0.0))
    dprob_t = jnp.dot(all_grads, own_values.T, preferred_element_type=jnp.float32)
    dscore_t = (prob_t * (dprob_t - all_delta[:, None])).astype(jnp.bfloat16)
    d_key = jnp.dot(dscore_t.T, all_queries, preferred_element_type=jnp.float32) * scale
    d_value = jnp.dot(prob_t.astype(jnp.bfloat16).T, all_grads, preferred_element_type=jnp.float32)

    kv_grad = lax.psum(jnp.stack([d_key, d_value], axis=0), "x").astype(jnp.bfloat16)
    kv_all = lax.all_gather(kv_grad, "g", axis=2, tiled=True)
    return (out, d_query.astype(jnp.bfloat16), kv_all[0], kv_all[1])


def solution(mesh):
    ctx_size = mesh.shape["ctx"]
    tp_size = mesh.shape["tp"]
    devices = np.asarray(mesh.devices).reshape(ctx_size, tp_size // GROUP, GROUP)
    inner = Mesh(devices, ("ctx", "g", "x"))
    heads = ("g", "x")
    return jax.shard_map(
        on_device,
        mesh=inner,
        in_specs=(
            P("ctx", heads),
            P("ctx", None),
            P("ctx", None),
            P("ctx"),
            P(heads, None, None),
            P(),
            P("ctx", heads),
        ),
        out_specs=(P("ctx", heads), P("ctx", heads), P("ctx", None), P("ctx", None)),
        check_vma=False,
    )
```

time: 878 us -> 287 us (0.33)
  the two profiles are of different devices: /device:TPU:4 before, /device:TPU:64 now
where the time goes in v1:
time: 287 us
  waiting for transfers between devices  135 us (47%)
  blocking collectives  104 us (36%)
  matrix products  25.6 us (9%)
  between operations  14.2 us (5%)
  local copies, waits for them, and re-layouts  6.13 us (2%)
    all_gather x1, waiting for transfers between devices, on_device(): every = lax.all_gather(packed, 'ctx', axis=0, tiled=True)  135 us
    all_gather x1, blocking collectives, on_device(): lax.all_gather(jnp.stack([lse, delta], axis=0), 'ctx', axis=1, tiled=True)  56.4 us
    all_gather x1, blocking collectives, on_device(): kv_all = lax.all_gather(kv_grad, 'g', axis=2, tiled=True)  29.1 us
    psum x1, blocking collectives, on_device(): lax.psum(jnp.stack([d_key, d_value], axis=0), 'x').astype(jnp.bfloat16)  18.3 us
  transfers between devices with their start and end apart: 1, of which 1 were waited for; matrix products, arithmetic and copies ran while one was open for 3% of the time, Pallas kernels for 0%

profile of v1, /device:TPU:64, one launch (start us, length us, event | category | flops | bytes accessed | tf_op | source)
XLA Modules:
  0.0 286.5 jit_solution(2966820536998513354)
XLA Ops:
  7.2 0.0 copy-start
  7.2 0.0 all-gather.2.cloned.1.call-start
  7.2 0.7 iota_compare_fusion.5
  8.0 0.8 bitcast_dynamic-update-slice_fusion.3
  8.8 0.8 bitcast_dynamic-update-slice_fusion.2
  9.5 0.8 bitcast_dynamic-update-slice_fusion.1
  10.3 0.8 bitcast_dynamic-update-slice_fusion
  11.1 0.0 copy-start.2
  11.1 0.7 copy-done.2
  11.7 0.0 all-gather.2.cloned.1.call-update
  11.8 0.9 copy.24
  12.7 0.0 copy-done
  12.7 0.8 fusion.36
  13.5 0.9 fusion.35
  14.4 1.0 fusion.34
  15.4 1.2 fusion.31
  16.6 1.5 fusion.12
  18.1 0.0 copy-start.3
  18.1 1.5 fusion.13
  19.7 135.3 %all-gather.2.cloned.1.call-done = bf16[4096,5,128]{2,0,1:T(8,128)(2,1)} async-done(((bf16[128,5,128]{2,0,1:T(8,128)(2,1)}), bf16[4096,5,128]{2,0,1:T(8,128)(2,1)}) %all-gather.2.cloned.1.call-update) | async-done | bytes 5242896 | tf_op jit(solution)/shard_map/all_gather | solution.py:30
  155.0 0.0 copy-done.3
  155.0 1.7 fusion.7
  156.6 2.7 fusion.59
  159.4 0.0 copy-start.1
  159.4 0.6 fusion.14
  160.0 2.1 multiply_reduce_fusion
  162.1 0.0 copy-done.1
  162.1 0.7 copy.30
  162.8 56.4 %all_gather.10 = f32[2,4096]{1,0:T(2,128)S(1)} all-gather(f32[2,128]{1,0:T(2,128)S(1)} %pad_maximum_fusion.1), channel_id=1, replica_groups=mesh['ctx'=32,'g'=6,'x'=4] {'ctx'}, dimensions={1}, use_global_device_ids=true | all-gather | bytes 33792 | tf_op jit(solution)/shard_map/all_gather | solution.py:63
  219.2 1.7 convolution_multiply_fusion
  220.9 2.7 fusion.3
  223.6 1.7 convolution_bitcast_fusion
  225.3 0.0 copy-start.4
  225.3 2.3 fusion.19
  227.7 18.3 %all-reduce.2 = bf16[2,128,128]{2,1,0:T(8,128)(2,1)S(1)} all-reduce(f32[2,128,128]{2,1,0:T(8,128)S(1)} %pad_maximum_fusion), channel_id=1, replica_groups=mesh['ctx'=32,'g'=6,'x'=4] {'x'}, use_global_device_ids=true, to_apply=%region_3.4 | all-reduce | flops 32768 | bytes 196608 | tf_op jit(solution)/shard_map/psum | solution.py:79
  246.0 29.1 %all_gather.11 = bf16[2,128,768]{2,1,0:T(8,128)(2,1)S(1)} all-gather(bf16[2,128,128]{2,1,0:T(8,128)(2,1)S(1)} %all-reduce.2), channel_id=1, replica_groups=mesh['ctx'=32,'g'=6,'x'=4] {'g'}, dimensions={2}, use_global_device_ids=true | all-gather | bytes 458752 | tf_op jit(solution)/shard_map/all_gather | solution.py:80
  275.1 0.8 slice_bitcast_fusion.17
  275.9 0.0 copy-done.4
  275.9 3.8 %fusion.21 = bf16[128,128]{1,0:T(8,128)(2,1)} fusion(bf16[128,128]{1,0:T(8,128)(2,1)S(1)} %copy-done.4, pred[128,4096]{1,0:T(32,128)(4,1)S(1)} %fusion.12, f32[128,4096]{1,0:T(8,128)} %copy-done.1, f32[128]{0:T(128)S(1)} %get-tuple-element.22, f32[128]{0:T(128)S(1)} %log_add_fusion, bf16[4096,5,128]{2,0,1:T(8,128)(2,1)} %all-gather.2.cloned.1.call-done), kind=kOutput, calls=%fused_computation.34 | convolution fusion | flops 271089664 | bytes 4785152 | tf_op jit(solution)/shard_map/dot_general | solution.py:61
  (7 shorter events, 0.1 us)
Async XLA Ops:
  7.2 5.5 %copy-start = (f32[1,16,16]{2,1,0:T(8,128)S(1)}, f32[1,16,16]{2,1,0:T(8,128)}, u32[]{:S(2)}) copy-start(f32[1,16,16]{2,1,0:T(8,128)} %param.11) | copy-start | bytes 3076
  7.2 147.8 %all-gather.2.cloned.1.call-start = ((), (), s32[]{:S(2)}) async-start(), calls=%async_computation | async-start | bytes 5406720 | tf_op jit(solution)/shard_map/all_gather | solution.py:30
  11.1 0.7 copy-start.2
  18.1 136.9 %copy-start.3 = (bf16[128,128]{1,0:T(8,128)(2,1)S(1)}, bf16[128,128]{1,0:T(8,128)(2,1)}, u32[]{:S(2)}) copy-start(bf16[128,128]{1,0:T(8,128)(2,1)} %param.7) | copy-start | bytes 98308
  159.4 2.7 copy-start.1
  225.3 50.5 %copy-start.4 = (bf16[128,128]{1,0:T(8,128)(2,1)S(1)}, bf16[128,128]{1,0:T(8,128)(2,1)}, u32[]{:S(2)}) copy-start(bf16[128,128]{1,0:T(8,128)(2,1)} %param.13) | copy-start | bytes 98308
Sparse Core Ops, SparseCore 0:
  12.5 142.4 all-gather.1

commit v2 on v1

--- a/solution.py
+++ b/solution.py
@@ -12,6 +12,43 @@
 BLK = 128
 NEG = -1e30
 HI = lax.Precision.HIGHEST
+
+
+def xor_pairs(count, bit):
+    return [(i, i ^ bit) for i in range(count)]
+
+
+def xor_gather(block, axis):
+    count = lax.axis_size(axis)
+    me = lax.axis_index(axis)
+    held = block[None]
+    bit = 1
+    while bit < count:
+        held = jnp.concatenate([held, lax.ppermute(held, axis, xor_pairs(count, bit))], axis=0)
+        bit *= 2
+    return jnp.take(held, me ^ jnp.arange(count), axis=0)
+
+
+def xor_sum(value, axis):
+    count = lax.axis_size(axis)
+    bit = 1
+    while bit < count:
+        value = value + lax.ppermute(value, axis, xor_pairs(count, bit))
+        bit *= 2
+    return value
+
+
+def bruck_gather(block, axis):
+    count = lax.axis_size(axis)
+    me = lax.axis_index(axis)
+    held = block[None]
+    step = 1
+    while step < count:
+        part = held[: min(step, count - step)]
+        pairs = [(i, (i - step) % count) for i in range(count)]
+        held = jnp.concatenate([held, lax.ppermute(part, axis, pairs)], axis=0)
+        step *= 2
+    return jnp.take(held, (jnp.arange(count) - me) % count, axis=0)
 
 
 def on_device(queries, keys, values, roles, role_table, block_mask, d_out):
@@ -60,9 +97,9 @@
     dscore = (prob * (dprob - delta[:, None])).astype(jnp.bfloat16)
     d_query = jnp.dot(dscore, all_keys, preferred_element_type=jnp.float32) * scale
 
-    stats = lax.all_gather(jnp.stack([lse, delta], axis=0), "ctx", axis=1, tiled=True)
-    all_lse = stats[0]
-    all_delta = stats[1]
+    stats = xor_gather(jnp.stack([lse, delta], axis=0), "ctx")
+    all_lse = stats[:, 0].reshape(total_rows)
+    all_delta = stats[:, 1].reshape(total_rows)
 
     k_open = jnp.dot(jnp.dot(all_block, mask_f, precision=HI), own_block.T, precision=HI) > 0.5
     k_allowed = (own_pos[None, :] <= pos[:, None]) & (
@@ -76,8 +113,9 @@
     d_key = jnp.dot(dscore_t.T, all_queries, preferred_element_type=jnp.float32) * scale
     d_value = jnp.dot(prob_t.astype(jnp.bfloat16).T, all_grads, preferred_element_type=jnp.float32)
 
-    kv_grad = lax.psum(jnp.stack([d_key, d_value], axis=0), "x").astype(jnp.bfloat16)
-    kv_all = lax.all_gather(kv_grad, "g", axis=2, tiled=True)
+    kv_grad = xor_sum(jnp.stack([d_key, d_value], axis=0), "x").astype(jnp.bfloat16)
+    kv_all = bruck_gather(kv_grad, "g")
+    kv_all = kv_all.transpose(1, 2, 0, 3).reshape(2, rows, -1)
     return (out, d_query.astype(jnp.bfloat16), kv_all[0], kv_all[1])
 
 

time: 287 us -> 257 us (0.90)
  the two profiles are of different devices: /device:TPU:64 before, /device:TPU:70 now
where the time goes in v2:
time: 257 us; the launch traced here: 256 us
  waiting for transfers between devices  172 us (67%)
  starting transfers between devices  31.9 us (12%)
  matrix products  27.6 us (11%)
  between operations  14.4 us (6%)
  local copies, waits for them, and re-layouts  8.67 us (3%)
    all_gather x1, waiting for transfers between devices, on_device(): every = lax.all_gather(packed, 'ctx', axis=0, tiled=True)  135 us
    ppermute x5, waiting for transfers between devices, xor_gather(): lax.ppermute(held, axis, xor_pairs(count, bit))  18.7 us
    ppermute x5, starting transfers between devices, xor_gather(): lax.ppermute(held, axis, xor_pairs(count, bit))  14.6 us
    ppermute x3, starting transfers between devices, bruck_gather(): held = jnp.concatenate([held, lax.ppermute(part, axis, pairs)], axis=0)  12.4 us
    ppermute x2, waiting for transfers between devices, xor_sum(): value = value + lax.ppermute(value, axis, xor_pairs(count, bit))  11.4 us
    unnamed x21, local copies, waits for them, and re-layouts  7.03 us
    ppermute x3, waiting for transfers between devices, bruck_gather(): held = jnp.concatenate([held, lax.ppermute(part, axis, pairs)], axis=0)  6.56 us
  transfers between devices with their start and end apart: 11, of which 9 were waited for; matrix products, arithmetic and copies ran while one was open for 6% of the time, Pallas kernels for 0%

profile of v2, /device:TPU:70, one launch (start us, length us, event | category | flops | bytes accessed | tf_op | source)
XLA Modules:
  0.0 256.4 jit_solution(15734983504762294187)
XLA Ops:
  7.2 0.0 copy-start
  7.2 0.0 all-gather.2.cloned.1.call-start
  7.2 0.7 iota_compare_fusion.5
  8.0 0.8 constant_dynamic-update-slice_fusion.3
  8.8 0.8 constant_dynamic-update-slice_fusion.2
  9.5 0.8 constant_dynamic-update-slice_fusion.1
  10.3 0.8 constant_dynamic-update-slice_fusion
  11.1 0.0 copy-start.2
  11.1 0.7 copy-done.2
  11.7 0.0 all-gather.2.cloned.1.call-update
  11.8 0.9 copy.28
  12.7 0.0 copy-done
  12.7 0.8 fusion.37
  13.6 0.9 fusion.36
  14.5 1.0 fusion.35
  15.5 1.2 fusion.31
  16.7 1.5 fusion.12
  18.2 0.0 copy-start.3
  18.2 1.5 fusion.13
  19.7 135.2 %all-gather.2.cloned.1.call-done = bf16[4096,5,128]{2,0,1:T(8,128)(2,1)} async-done(((bf16[128,5,128]{2,0,1:T(8,128)(2,1)}), bf16[4096,5,128]{2,0,1:T(8,128)(2,1)}) %all-gather.2.cloned.1.call-update) | async-done | bytes 5242896 | tf_op jit(solution)/shard_map/all_gather | solution.py:67
  154.9 0.0 copy-done.3
  154.9 1.7 fusion.7
  156.6 2.7 %fusion.64 = (f32[128]{0:T(128)S(1)}, f32[128,4096]{1,0:T(8,128)S(1)}) fusion(pred[128,4096]{1,0:T(32,128)(4,1)S(1)} %fusion.12, f32[128,4096]{1,0:T(8,128)S(1)} %fusion.7, f32[128,16]{0,1:T(8,128)S(1)} %fusion.37, bf16[4096,5,128]{2,0,1:T(8,128)(2,1)} %all-gather.2.cloned.1.call-done), kind=kOutput, calls=%fused_computation.131 | convolution fusion | flops 102236032 | bytes 5775872 | tf_op jit(solution)/shard_map/dot_general | solution.py:85
  159.3 0.0 copy-start.1
  159.3 0.6 fusion.14
  160.0 2.1 multiply_reduce_fusion
  162.0 0.0 copy-done.1
  162.0 2.1 collective-permute-start
  164.2 0.9 collective-permute-done
  165.1 2.6 %collective-permute-start.1 = (f32[2,2,128]{2,1,0:T(2,128)S(1)}, f32[2,2,128]{2,1,0:T(2,128)S(1)}, u32[]{:S(2)}, u32[]{:S(2)}) collective-permute-start(f32[2,2,128]{2,1,0:T(2,128)S(1)} %pad_maximum_fusion.5), channel_id=1, source_target_pairs={{0,48},{24,72},{48,0},{72,24},{96,144},{120,168},{144,96},{168,120... | collective-permute-start | bytes 6152 | tf_op jit(solution)/shard_map/ppermute | solution.py:27
  167.8 2.8 %collective-permute-done.1 = f32[2,2,128]{2,1,0:T(2,128)S(1)} collective-permute-done((f32[2,2,128]{2,1,0:T(2,128)S(1)}, f32[2,2,128]{2,1,0:T(2,128)S(1)}, u32[]{:S(2)}, u32[]{:S(2)}) %collective-permute-start.1) | collective-permute-done | bytes 2080 | tf_op jit(solution)/shard_map/ppermute | solution.py:27
  170.6 3.3 %collective-permute-start.2 = (f32[4,2,128]{2,1,0:T(2,128)S(1)}, f32[4,2,128]{2,1,0:T(2,128)S(1)}, u32[]{:S(2)}, u32[]{:S(2)}) collective-permute-start(f32[4,2,128]{2,1,0:T(2,128)S(1)} %pad_maximum_fusion.4), channel_id=1, source_target_pairs={{0,96},{24,120},{48,144},{72,168},{96,0},{120,24},{144,48},{168,72... | collective-permute-start | bytes 12296 | tf_op jit(solution)/shard_map/ppermute | solution.py:27
  173.9 3.0 %collective-permute-done.2 = f32[4,2,128]{2,1,0:T(2,128)S(1)} collective-permute-done((f32[4,2,128]{2,1,0:T(2,128)S(1)}, f32[4,2,128]{2,1,0:T(2,128)S(1)}, u32[]{:S(2)}, u32[]{:S(2)}) %collective-permute-start.2) | collective-permute-done | bytes 4128 | tf_op jit(solution)/shard_map/ppermute | solution.py:27
  177.0 4.6 %collective-permute-start.3 = (f32[8,2,128]{2,1,0:T(2,128)S(1)}, f32[8,2,128]{2,1,0:T(2,128)S(1)}, u32[]{:S(2)}, u32[]{:S(2)}) collective-permute-start(f32[8,2,128]{2,1,0:T(2,128)S(1)} %pad_maximum_fusion.3), channel_id=1, source_target_pairs={{0,192},{24,216},{48,240},{72,264},{96,288},{120,312},{144,336},{1... | collective-permute-start | bytes 24584 | tf_op jit(solution)/shard_map/ppermute | solution.py:27
  181.6 4.8 %collective-permute-done.3 = f32[8,2,128]{2,1,0:T(2,128)S(1)} collective-permute-done((f32[8,2,128]{2,1,0:T(2,128)S(1)}, f32[8,2,128]{2,1,0:T(2,128)S(1)}, u32[]{:S(2)}, u32[]{:S(2)}) %collective-permute-start.3) | collective-permute-done | bytes 8224 | tf_op jit(solution)/shard_map/ppermute | solution.py:27
  186.4 1.9 collective-permute-start.4
  188.4 3.1 %convolution_multiply_fusion = f32[4096,128]{0,1:T(8,128)} fusion(bf16[4096,5,128]{2,0,1:T(8,128)(2,1)} %all-gather.2.cloned.1.call-done, bf16[128,768]{1,0:T(8,128)(2,1)} %param.8, s32[]{:T(128)S(6)} %select_n.126), kind=kOutput, calls=%fused_computation.8 | convolution fusion | flops 134742016 | bytes 3178500 | tf_op jit(solution)/shard_map/dot_general | solution.py:109
  191.4 7.1 %collective-permute-done.4 = f32[16,2,128]{2,1,0:T(2,128)S(1)} collective-permute-done((f32[16,2,128]{2,1,0:T(2,128)S(1)}, f32[16,2,128]{2,1,0:T(2,128)S(1)}, u32[]{:S(2)}, u32[]{:S(2)}) %collective-permute-start.4) | collective-permute-done | bytes 16416 | tf_op jit(solution)/shard_map/ppermute | solution.py:27
  198.5 0.6 gather_fusion
  199.1 0.1 broadcast_select_fusion
  199.3 3.4 %fusion.3 = f32[4096,128]{0,1:T(8,128)S(1)} fusion(pred[4096,128]{0,1:T(32,128)(4,1)S(1)} %fusion.13, f32[4096,128]{0,1:T(8,128)} %convolution_multiply_fusion, f32[128,16]{0,1:T(8,128)S(1)} %fusion.36, f32[4096]{0:T(1024)S(1)} %bitcast.90, bf16[4096,5,128]{2,0,1:T(8,128)(2,1)} %all-gather.2.cloned.1.call-done), kind=kOutput, calls=%fused_computation.7 | convolution fusion | flops 102236160 | bytes 5791744 | tf_op jit(solution)/shard_map/dot_general | solution.py:108
  202.7 1.7 convolution_bitcast_fusion
  204.3 0.0 copy-start.4
  204.4 2.3 fusion.19
  206.7 2.8 %collective-permute-start.5 = (f32[2,128,128]{2,1,0:T(8,128)S(1)}, f32[2,128,128]{2,1,0:T(8,128)S(1)}, u32[]{:S(2)}, u32[]{:S(2)}) collective-permute-start(f32[2,128,128]{2,1,0:T(8,128)S(1)} %pad_maximum_fusion.1), channel_id=1, source_target_pairs={{0,1},{1,0},{2,3},{3,2},{4,5},{5,4},{6,7},{7,6},{8,9},{9,8},{10,11... | collective-permute-start | bytes 393224 | tf_op jit(solution)/shard_map/ppermute | solution.py:36
  209.5 5.3 %collective-permute-done.5 = f32[2,128,128]{2,1,0:T(8,128)S(1)} collective-permute-done((f32[2,128,128]{2,1,0:T(8,128)S(1)}, f32[2,128,128]{2,1,0:T(8,128)S(1)}, u32[]{:S(2)}, u32[]{:S(2)}) %collective-permute-start.5) | collective-permute-done | bytes 131104 | tf_op jit(solution)/shard_map/ppermute | solution.py:36
  214.8 2.2 collective-permute-start.6
  217.0 6.2 %collective-permute-done.6 = f32[2,128,128]{2,1,0:T(8,128)S(1)} collective-permute-done((f32[2,128,128]{2,1,0:T(8,128)S(1)}, f32[2,128,128]{2,1,0:T(8,128)S(1)}, u32[]{:S(2)}, u32[]{:S(2)}) %collective-permute-start.6) | collective-permute-done | bytes 131104 | tf_op jit(solution)/shard_map/ppermute | solution.py:36
  223.2 2.6 %collective-permute-start.7 = (bf16[1,2,128,128]{3,2,1,0:T(8,128)(2,1)S(1)}, bf16[1,2,128,128]{3,2,1,0:T(8,128)(2,1)S(1)}, u32[]{:S(2)}, u32[]{:S(2)}) collective-permute-start(bf16[1,2,128,128]{3,2,1,0:T(8,128)(2,1)S(1)} %fusion.34), channel_id=1, source_target_pairs={{0,20},{4,0},{8,4},{12,8},{16,12},{20,16},{1,21},{5,1},{9,5},{13,9... | collective-permute-start | bytes 196616 | tf_op jit(solution)/shard_map/ppermute | solution.py:49
  225.8 6.6 %collective-permute-done.7 = bf16[1,2,128,128]{3,2,1,0:T(8,128)(2,1)S(1)} collective-permute-done((bf16[1,2,128,128]{3,2,1,0:T(8,128)(2,1)S(1)}, bf16[1,2,128,128]{3,2,1,0:T(8,128)(2,1)S(1)}, u32[]{:S(2)}, u32[]{:S(2)}) %collective-permute-start.7) | collective-permute-done | bytes 65568 | tf_op jit(solution)/shard_map/ppermute | solution.py:49
  232.4 1.9 collective-permute-start.9
  234.3 7.8 %collective-permute-start.8 = (bf16[2,2,128,128]{3,2,1,0:T(8,128)(2,1)S(1)}, bf16[2,2,128,128]{3,2,1,0:T(8,128)(2,1)S(1)}, u32[]{:S(2)}, u32[]{:S(2)}) collective-permute-start(bf16[2,2,128,128]{3,2,1,0:T(8,128)(2,1)S(1)} %pad_maximum_fusion.2), channel_id=1, source_target_pairs={{0,16},{4,20},{8,0},{12,4},{16,8},{20,12},{1,17},{5,21},{9,1},{13,... | collective-permute-start | bytes 393224 | tf_op jit(solution)/shard_map/ppermute | solution.py:49
  242.1 0.0 copy-done.4
  242.1 3.8 %fusion.21 = bf16[128,128]{1,0:T(8,128)(2,1)} fusion(bf16[128,128]{1,0:T(8,128)(2,1)S(1)} %copy-done.4, pred[128,4096]{1,0:T(32,128)(4,1)S(1)} %fusion.12, f32[128,4096]{1,0:T(8,128)} %copy-done.1, f32[128]{0:T(128)S(1)} %get-tuple-element.32, f32[128]{0:T(128)S(1)} %log_add_fusion, bf16[4096,5,128]{2,0,1:T(8,128)(2,1)} %all-gather.2.cloned.1.call-done), kind=kOutput, calls=%fused_computation.36 | convolution fusion | flops 271089664 | bytes 4785152 | tf_op jit(solution)/shard_map/dot_general | solution.py:98
  246.0 0.7 copy.36
  246.7 0.0 collective-permute-done.9
  246.7 0.0 collective-permute-done.8
  246.7 0.6 gather_fusion.1
  247.4 0.1 select_bitcast_fusion
  247.5 0.2 copy.34
  247.7 0.8 copy.37
  248.5 0.2 copy.35
  248.7 0.8 copy.38
  (27 shorter events, 0.4 us)
Async XLA Ops:
  7.2 5.6 %copy-start = (f32[1,16,16]{2,1,0:T(8,128)S(1)}, f32[1,16,16]{2,1,0:T(8,128)}, u32[]{:S(2)}) copy-start(f32[1,16,16]{2,1,0:T(8,128)} %param.11) | copy-start | bytes 3076
  7.2 147.7 %all-gather.2.cloned.1.call-start = ((), (), s32[]{:S(2)}) async-start(), calls=%async_computation | async-start | bytes 5406720 | tf_op jit(solution)/shard_map/all_gather | solution.py:67
  11.1 0.7 copy-start.2
  18.2 136.7 %copy-start.3 = (bf16[128,128]{1,0:T(8,128)(2,1)S(1)}, bf16[128,128]{1,0:T(8,128)(2,1)}, u32[]{:S(2)}) copy-start(bf16[128,128]{1,0:T(8,128)(2,1)} %param.7) | copy-start | bytes 98308
  159.3 2.7 %copy-start.1 = (f32[128,4096]{1,0:T(8,128)}, f32[128,4096]{1,0:T(8,128)S(1)}, u32[]{:S(2)}) copy-start(f32[128,4096]{1,0:T(8,128)S(1)} %get-tuple-element.31) | copy-start | bytes 6291460
  162.0 3.1 %collective-permute-start = (f32[1,2,128]{2,1,0:T(2,128)S(1)}, f32[1,2,128]{2,1,0:T(2,128)S(1)}, u32[]{:S(2)}, u32[]{:S(2)}) collective-permute-start(f32[1,2,128]{2,1,0:T(2,128)S(1)} %maximum_bitcast_fusion), channel_id=1, source_target_pairs={{0,24},{24,0},{48,72},{72,48},{96,120},{120,96},{144,168},{168,144... | collective-permute-start | bytes 3080 | tf_op jit(solution)/shard_map/ppermute | solution.py:27
  165.1 5.5 %collective-permute-start.1 = (f32[2,2,128]{2,1,0:T(2,128)S(1)}, f32[2,2,128]{2,1,0:T(2,128)S(1)}, u32[]{:S(2)}, u32[]{:S(2)}) collective-permute-start(f32[2,2,128]{2,1,0:T(2,128)S(1)} %pad_maximum_fusion.5), channel_id=1, source_target_pairs={{0,48},{24,72},{48,0},{72,24},{96,144},{120,168},{144,96},{168,120... | collective-permute-start | bytes 6152 | tf_op jit(solution)/shard_map/ppermute | solution.py:27
  170.6 6.4 %collective-permute-start.2 = (f32[4,2,128]{2,1,0:T(2,128)S(1)}, f32[4,2,128]{2,1,0:T(2,128)S(1)}, u32[]{:S(2)}, u32[]{:S(2)}) collective-permute-start(f32[4,2,128]{2,1,0:T(2,128)S(1)} %pad_maximum_fusion.4), channel_id=1, source_target_pairs={{0,96},{24,120},{48,144},{72,168},{96,0},{120,24},{144,48},{168,72... | collective-permute-start | bytes 12296 | tf_op jit(solution)/shard_map/ppermute | solution.py:27
  177.0 9.4 %collective-permute-start.3 = (f32[8,2,128]{2,1,0:T(2,128)S(1)}, f32[8,2,128]{2,1,0:T(2,128)S(1)}, u32[]{:S(2)}, u32[]{:S(2)}) collective-permute-start(f32[8,2,128]{2,1,0:T(2,128)S(1)} %pad_maximum_fusion.3), channel_id=1, source_target_pairs={{0,192},{24,216},{48,240},{72,264},{96,288},{120,312},{144,336},{1... | collective-permute-start | bytes 24584 | tf_op jit(solution)/shard_map/ppermute | solution.py:27
  186.4 12.1 %collective-permute-start.4 = (f32[16,2,128]{2,1,0:T(2,128)S(1)}, f32[16,2,128]{2,1,0:T(2,128)S(1)}, u32[]{:S(2)}, u32[]{:S(2)}) collective-permute-start(f32[16,2,128]{2,1,0:T(2,128)S(1)} %get-tuple-element.20), channel_id=1, source_target_pairs={{0,384},{24,408},{48,432},{72,456},{96,480},{120,504},{144,528},{1... | collective-permute-start | bytes 49160 | tf_op jit(solution)/shard_map/ppermute | solution.py:27
  204.3 37.8 %copy-start.4 = (bf16[128,128]{1,0:T(8,128)(2,1)S(1)}, bf16[128,128]{1,0:T(8,128)(2,1)}, u32[]{:S(2)}) copy-start(bf16[128,128]{1,0:T(8,128)(2,1)} %param.13) | copy-start | bytes 98308
  206.7 8.0 %collective-permute-start.5 = (f32[2,128,128]{2,1,0:T(8,128)S(1)}, f32[2,128,128]{2,1,0:T(8,128)S(1)}, u32[]{:S(2)}, u32[]{:S(2)}) collective-permute-start(f32[2,128,128]{2,1,0:T(8,128)S(1)} %pad_maximum_fusion.1), channel_id=1, source_target_pairs={{0,1},{1,0},{2,3},{3,2},{4,5},{5,4},{6,7},{7,6},{8,9},{9,8},{10,11... | collective-permute-start | bytes 393224 | tf_op jit(solution)/shard_map/ppermute | solution.py:36
  214.8 8.4 %collective-permute-start.6 = (f32[2,128,128]{2,1,0:T(8,128)S(1)}, f32[2,128,128]{2,1,0:T(8,128)S(1)}, u32[]{:S(2)}, u32[]{:S(2)}) collective-permute-start(f32[2,128,128]{2,1,0:T(8,128)S(1)} %fusion.61), channel_id=1, source_target_pairs={{0,2},{1,3},{2,0},{3,1},{4,6},{5,7},{6,4},{7,5},{8,10},{9,11},{10,... | collective-permute-start | bytes 393224 | tf_op jit(solution)/shard_map/ppermute | solution.py:36
  223.2 9.2 %collective-permute-start.7 = (bf16[1,2,128,128]{3,2,1,0:T(8,128)(2,1)S(1)}, bf16[1,2,128,128]{3,2,1,0:T(8,128)(2,1)S(1)}, u32[]{:S(2)}, u32[]{:S(2)}) collective-permute-start(bf16[1,2,128,128]{3,2,1,0:T(8,128)(2,1)S(1)} %fusion.34), channel_id=1, source_target_pairs={{0,20},{4,0},{8,4},{12,8},{16,12},{20,16},{1,21},{5,1},{9,5},{13,9... | collective-permute-start | bytes 196616 | tf_op jit(solution)/shard_map/ppermute | solution.py:49
  232.4 14.3 %collective-permute-start.9 = (bf16[2,2,128,128]{3,2,1,0:T(8,128)(2,1)S(1)}, bf16[2,2,128,128]{3,2,1,0:T(8,128)(2,1)S(1)}, u32[]{:S(2)}, u32[]{:S(2)}) collective-permute-start(bf16[2,2,128,128]{3,2,1,0:T(8,128)(2,1)S(1)} %pad_maximum_fusion.2), channel_id=1, source_target_pairs={{0,8},{4,12},{8,16},{12,20},{16,0},{20,4},{1,9},{5,13},{9,17},{13,... | collective-permute-start | bytes 393224 | tf_op jit(solution)/shard_map/ppermute | solution.py:49
  234.3 12.4 %collective-permute-start.8 = (bf16[2,2,128,128]{3,2,1,0:T(8,128)(2,1)S(1)}, bf16[2,2,128,128]{3,2,1,0:T(8,128)(2,1)S(1)}, u32[]{:S(2)}, u32[]{:S(2)}) collective-permute-start(bf16[2,2,128,128]{3,2,1,0:T(8,128)(2,1)S(1)} %pad_maximum_fusion.2), channel_id=1, source_target_pairs={{0,16},{4,20},{8,0},{12,4},{16,8},{20,12},{1,17},{5,21},{9,1},{13,... | collective-permute-start | bytes 393224 | tf_op jit(solution)/shard_map/ppermute | solution.py:49
Sparse Core Ops, SparseCore 0:
  12.5 142.3 all-gather.1

commit v3 on v2

--- a/solution.py
+++ b/solution.py
@@ -51,11 +51,52 @@
     return jnp.take(held, (jnp.arange(count) - me) % count, axis=0)
 
 
+def shift_pairs(count, step):
+    return [(i, (i + step) % count) for i in range(count)]
+
+
+def gather_ctx(block):
+    zh = lax.axis_index("zh")
+    y = lax.axis_index("y")
+    core = lax.axis_index("core")
+    ny = lax.axis_size("y")
+    ncore = lax.axis_size("core")
+    nz = lax.axis_size("zh")
+
+    def index_of(z, yy, cc):
+        return (z * ny + yy) * ncore + cc
+
+    held = [block[None], lax.ppermute(block[None], "zh", xor_pairs(nz, 1))]
+    chip = jnp.concatenate(held, axis=0)
+    blocks = [chip]
+    owners = [jnp.stack([index_of(zh, y, core), index_of(1 - zh, y, core)])]
+    left = chip
+    right = chip
+    for step in range(1, ny // 2 + 1):
+        left = lax.ppermute(left, "y", shift_pairs(ny, 1))
+        blocks.append(left)
+        yy = (y - step) % ny
+        owners.append(jnp.stack([index_of(zh, yy, core), index_of(1 - zh, yy, core)]))
+        if step < ny - step:
+            right = lax.ppermute(right, "y", shift_pairs(ny, -1))
+            blocks.append(right)
+            yy = (y + step) % ny
+            owners.append(jnp.stack([index_of(zh, yy, core), index_of(1 - zh, yy, core)]))
+    mine = jnp.concatenate(blocks, axis=0)
+    owner = jnp.concatenate(owners, axis=0)
+    other = lax.ppermute(mine, "core", xor_pairs(ncore, 1))
+    every = jnp.concatenate([mine, other], axis=0)
+    owner = jnp.concatenate([owner, owner - core + (1 - core)], axis=0)
+    return every, owner
+
+
 def on_device(queries, keys, values, roles, role_table, block_mask, d_out):
     rows = queries.shape[0]
     role_count = role_table.shape[1]
     scale = 1.0 / math.sqrt(HS)
-    ctx_index = lax.axis_index("ctx")
+    ctx_index = (lax.axis_index("zh") * lax.axis_size("y") + lax.axis_index("y")) * lax.axis_size(
+        "core"
+    ) + lax.axis_index("core")
     group = lax.axis_index("g")
     own_keys = lax.dynamic_slice_in_dim(keys, group * HS, HS, 1)
     own_values = lax.dynamic_slice_in_dim(values, group * HS, HS, 1)
@@ -64,7 +105,8 @@
     role_onehot = (roles[:, None] == jnp.arange(role_count)[None, :]).astype(jnp.float32)
     role_slot = jnp.pad(role_onehot, ((0, 0), (0, HS - role_count))).astype(jnp.bfloat16)
     packed = jnp.stack([own_keys, own_values, queries, d_out, role_slot], axis=1)
-    every = lax.all_gather(packed, "ctx", axis=0, tiled=True)
+    every, owner = gather_ctx(packed)
+    every = every.reshape((-1,) + packed.shape[1:])
     total_rows = every.shape[0]
     all_keys = every[:, 0]
     all_values = every[:, 1]
@@ -72,7 +114,7 @@
     all_grads = every[:, 3]
     all_onehot = every[:, 4, :role_count].astype(jnp.float32)
 
-    pos = jnp.arange(total_rows)
+    pos = (owner[:, None] * rows + jnp.arange(rows)[None, :]).reshape(total_rows)
     own_pos = ctx_index * rows + jnp.arange(rows)
     mask_f = block_mask.astype(jnp.float32)
     all_block = (pos[:, None] // BLK == jnp.arange(block_mask.shape[0])[None, :]).astype(jnp.float32)
@@ -97,7 +139,7 @@
     dscore = (prob * (dprob - delta[:, None])).astype(jnp.bfloat16)
     d_query = jnp.dot(dscore, all_keys, preferred_element_type=jnp.float32) * scale
 
-    stats = xor_gather(jnp.stack([lse, delta], axis=0), "ctx")
+    stats = jnp.take(xor_gather(jnp.stack([lse, delta], axis=0), ("zh", "y", "core")), owner, axis=0)
     all_lse = stats[:, 0].reshape(total_rows)
     all_delta = stats[:, 1].reshape(total_rows)
 
@@ -123,20 +165,21 @@
     ctx_size = mesh.shape["ctx"]
     tp_size = mesh.shape["tp"]
     devices = np.asarray(mesh.devices).reshape(ctx_size, tp_size // GROUP, GROUP)
-    inner = Mesh(devices, ("ctx", "g", "x"))
+    inner = Mesh(devices.reshape(2, ctx_size // 4, 2, tp_size // GROUP, GROUP), ("zh", "y", "core", "g", "x"))
     heads = ("g", "x")
+    seq = ("zh", "y", "core")
     return jax.shard_map(
         on_device,
         mesh=inner,
         in_specs=(
-            P("ctx", heads),
-            P("ctx", None),
-            P("ctx", None),
-            P("ctx"),
+            P(seq, heads),
+            P(seq, None),
+            P(seq, None),
+            P(seq),
             P(heads, None, None),
             P(),
-            P("ctx", heads),
+            P(seq, heads),
         ),
-        out_specs=(P("ctx", heads), P("ctx", heads), P("ctx", None), P("ctx", None)),
+        out_specs=(P(seq, heads), P(seq, heads), P(seq, None), P(seq, None)),
         check_vma=False,
     )

time: 257 us -> 187 us (0.73)
  the two profiles are of different devices: /device:TPU:70 before, /device:TPU:4 now
where the time goes in v3:
time: 187 us; the launch traced here: 186 us
  starting transfers between devices  96 us (51%)
  waiting for transfers between devices  42.7 us (23%)
  matrix products  25.6 us (14%)
  local copies, waits for them, and re-layouts  18.4 us (10%)
  other arithmetic  2.15 us (1%)
    ppermute x3, starting transfers between devices, bruck_gather(): held = jnp.concatenate([held, lax.ppermute(part, axis, pairs)], axis=0)  24.1 us
    ppermute x5, starting transfers between devices, xor_gather(): lax.ppermute(held, axis, xor_pairs(count, bit))  22.9 us
    ppermute x1, starting transfers between devices, gather_ctx(): held = [block[None], lax.ppermute(block[None], 'zh', xor_pairs(nz, 1))]  15.1 us
    ppermute x3, starting transfers between devices, gather_ctx(): right = lax.ppermute(right, 'y', shift_pairs(ny, -1))  14.4 us
    unnamed x33, local copies, waits for them, and re-layouts  13 us
    ppermute x4, waiting for transfers between devices, gather_ctx(): left = lax.ppermute(left, 'y', shift_pairs(ny, 1))  12.7 us
    ppermute x5, waiting for transfers between devices, xor_gather(): lax.ppermute(held, axis, xor_pairs(count, bit))  11.2 us
    ppermute x4, starting transfers between devices, gather_ctx(): left = lax.ppermute(left, 'y', shift_pairs(ny, 1))  9.21 us
  transfers between devices with their start and end apart: 19, of which 14 were waited for; matrix products, arithmetic and copies ran while one was open for 11% of the time, Pallas kernels for 0%

profile of v3, /device:TPU:4, one launch (start us, length us, event | category | flops | bytes accessed | tf_op | source)
XLA Modules:
  0.0 186.0 jit_solution(2176442255718352367)
XLA Ops:
  0.7 0.7 iota_compare_fusion.3
  1.4 0.8 constant_dynamic-update-slice_fusion.4
  2.2 0.8 constant_dynamic-update-slice_fusion.3
  2.9 0.8 constant_dynamic-update-slice_fusion.2
  3.7 0.8 constant_dynamic-update-slice_fusion.1
  4.5 15.1 %collective-permute-start = (bf16[1,128,5,128]{3,1,0,2:T(8,128)(2,1)S(1)}, bf16[1,128,5,128]{3,1,0,2:T(8,128)(2,1)S(1)}, u32[]{:S(2)}, u32[]{:S(2)}) collective-permute-start(bf16[1,128,5,128]{3,1,0,2:T(8,128)(2,1)S(1)} %bitcast.129), channel_id=1, source_target_pairs={{0,384},{384,0},{1,385},{385,1},{2,386},{386,2},{3,387},{387,3},{4... | collective-permute-start | bytes 491528 | tf_op jit(solution)/shard_map/ppermute | solution.py:69
  19.9 4.1 %collective-permute-done = bf16[1,128,5,128]{3,1,0,2:T(8,128)(2,1)S(1)} collective-permute-done((bf16[1,128,5,128]{3,1,0,2:T(8,128)(2,1)S(1)}, bf16[1,128,5,128]{3,1,0,2:T(8,128)(2,1)S(1)}, u32[]{:S(2)}, u32[]{:S(2)}) %collective-permute-start) | collective-permute-done | bytes 163872 | tf_op jit(solution)/shard_map/ppermute | solution.py:69
  24.1 3.5 %collective-permute-start.1 = (bf16[2,128,5,128]{3,1,0,2:T(8,128)(2,1)S(1)}, bf16[2,128,5,128]{3,1,0,2:T(8,128)(2,1)S(1)}, u32[]{:S(2)}, u32[]{:S(2)}) collective-permute-start(bf16[2,128,5,128]{3,1,0,2:T(8,128)(2,1)S(1)} %pad_maximum_fusion.1), channel_id=1, source_target_pairs={{0,48},{48,96},{96,144},{144,192},{192,240},{240,288},{288,336},{3... | collective-permute-start | bytes 983048 | tf_op jit(solution)/shard_map/ppermute | solution.py:76
  27.6 0.8 constant_dynamic-update-slice_fusion.13
  28.3 3.8 %collective-permute-start.2 = (bf16[2,128,5,128]{3,1,0,2:T(8,128)(2,1)S(1)}, bf16[2,128,5,128]{3,1,0,2:T(8,128)(2,1)S(1)}, u32[]{:S(2)}, u32[]{:S(2)}) collective-permute-start(bf16[2,128,5,128]{3,1,0,2:T(8,128)(2,1)S(1)} %pad_maximum_fusion.1), channel_id=1, source_target_pairs={{0,336},{48,0},{96,48},{144,96},{192,144},{240,192},{288,240},{336... | collective-permute-start | bytes 983048 | tf_op jit(solution)/shard_map/ppermute | solution.py:81
  32.1 4.2 %collective-permute-done.1 = bf16[2,128,5,128]{3,1,0,2:T(8,128)(2,1)S(1)} collective-permute-done((bf16[2,128,5,128]{3,1,0,2:T(8,128)(2,1)S(1)}, bf16[2,128,5,128]{3,1,0,2:T(8,128)(2,1)S(1)}, u32[]{:S(2)}, u32[]{:S(2)}) %collective-permute-start.1) | collective-permute-done | bytes 327712 | tf_op jit(solution)/shard_map/ppermute | solution.py:76
  36.4 1.9 %collective-permute-start.3 = (bf16[2,128,5,128]{3,1,0,2:T(8,128)(2,1)S(1)}, bf16[2,128,5,128]{3,1,0,2:T(8,128)(2,1)S(1)}, u32[]{:S(2)}, u32[]{:S(2)}) collective-permute-start(bf16[2,128,5,128]{3,1,0,2:T(8,128)(2,1)S(1)} %collective-permute-done.1), channel_id=1, source_target_pairs={{0,48},{48,96},{96,144},{144,192},{192,240},{240,288},{288,336},{3... | collective-permute-start | bytes 983048 | tf_op jit(solution)/shard_map/ppermute | solution.py:76
  38.6 5.3 %collective-permute-start.4 = (bf16[2,128,5,128]{3,1,0,2:T(8,128)(2,1)S(1)}, bf16[2,128,5,128]{3,1,0,2:T(8,128)(2,1)S(1)}, u32[]{:S(2)}, u32[]{:S(2)}) collective-permute-start(bf16[2,128,5,128]{3,1,0,2:T(8,128)(2,1)S(1)} %collective-permute-done.2), channel_id=1, source_target_pairs={{0,336},{48,0},{96,48},{144,96},{192,144},{240,192},{288,240},{336... | collective-permute-start | bytes 983048 | tf_op jit(solution)/shard_map/ppermute | solution.py:81
  43.9 0.8 constant_dynamic-update-slice_fusion.12
  44.7 2.9 %collective-permute-done.3 = bf16[2,128,5,128]{3,1,0,2:T(8,128)(2,1)S(1)} collective-permute-done((bf16[2,128,5,128]{3,1,0,2:T(8,128)(2,1)S(1)}, bf16[2,128,5,128]{3,1,0,2:T(8,128)(2,1)S(1)}, u32[]{:S(2)}, u32[]{:S(2)}) %collective-permute-start.3) | collective-permute-done | bytes 327712 | tf_op jit(solution)/shard_map/ppermute | solution.py:76
  47.6 1.9 %collective-permute-start.5 = (bf16[2,128,5,128]{3,1,0,2:T(8,128)(2,1)S(1)}, bf16[2,128,5,128]{3,1,0,2:T(8,128)(2,1)S(1)}, u32[]{:S(2)}, u32[]{:S(2)}) collective-permute-start(bf16[2,128,5,128]{3,1,0,2:T(8,128)(2,1)S(1)} %collective-permute-done.3), channel_id=1, source_target_pairs={{0,48},{48,96},{96,144},{144,192},{192,240},{240,288},{288,336},{3... | collective-permute-start | bytes 983048 | tf_op jit(solution)/shard_map/ppermute | solution.py:76
  49.5 1.0 constant_dynamic-update-slice_fusion.11
  50.5 1.0 constant_dynamic-update-slice_fusion.10
  51.4 5.3 %collective-permute-start.6 = (bf16[2,128,5,128]{3,1,0,2:T(8,128)(2,1)S(1)}, bf16[2,128,5,128]{3,1,0,2:T(8,128)(2,1)S(1)}, u32[]{:S(2)}, u32[]{:S(2)}) collective-permute-start(bf16[2,128,5,128]{3,1,0,2:T(8,128)(2,1)S(1)} %collective-permute-done.4), channel_id=1, source_target_pairs={{0,336},{48,0},{96,48},{144,96},{192,144},{240,192},{288,240},{336... | collective-permute-start | bytes 983048 | tf_op jit(solution)/shard_map/ppermute | solution.py:81
  56.7 1.0 constant_dynamic-update-slice_fusion.9
  57.9 1.9 %collective-permute-start.7 = (bf16[2,128,5,128]{3,1,0,2:T(8,128)(2,1)S(1)}, bf16[2,128,5,128]{3,1,0,2:T(8,128)(2,1)S(1)}, u32[]{:S(2)}, u32[]{:S(2)}) collective-permute-start(bf16[2,128,5,128]{3,1,0,2:T(8,128)(2,1)S(1)} %collective-permute-done.5), channel_id=1, source_target_pairs={{0,48},{48,96},{96,144},{144,192},{192,240},{240,288},{288,336},{3... | collective-permute-start | bytes 983048 | tf_op jit(solution)/shard_map/ppermute | solution.py:76
  59.8 1.0 constant_dynamic-update-slice_fusion.8
  60.8 1.0 constant_dynamic-update-slice_fusion.7
  61.8 1.0 constant_dynamic-update-slice_fusion.6
  62.7 5.3 %collective-permute-done.7 = bf16[2,128,5,128]{3,1,0,2:T(8,128)(2,1)S(1)} collective-permute-done((bf16[2,128,5,128]{3,1,0,2:T(8,128)(2,1)S(1)}, bf16[2,128,5,128]{3,1,0,2:T(8,128)(2,1)S(1)}, u32[]{:S(2)}, u32[]{:S(2)}) %collective-permute-start.7) | collective-permute-done | bytes 327712 | tf_op jit(solution)/shard_map/ppermute | solution.py:76
  68.1 1.0 constant_dynamic-update-slice_fusion.5
  69.0 1.9 %collective-permute-start.8 = (bf16[16,128,5,128]{3,1,0,2:T(8,128)(2,1)}, bf16[16,128,5,128]{3,1,0,2:T(8,128)(2,1)S(1)}, u32[]{:S(2)}, u32[]{:S(2)}) collective-permute-start(bf16[16,128,5,128]{3,1,0,2:T(8,128)(2,1)} %get-tuple-element.19), channel_id=1, source_target_pairs={{0,24},{24,0},{1,25},{25,1},{2,26},{26,2},{3,27},{27,3},{4,28},{28... | collective-permute-start | bytes 7864328 | tf_op jit(solution)/shard_map/ppermute | solution.py:87
  72.2 0.5 fusion.31
  72.6 1.4 fusion.12
  74.1 2.2 %fusion.13 = pred[4096,128]{0,1:T(32,128)(4,1)} fusion(f32[4096,32]{0,1:T(8,128)S(1)} %fusion.31, s32[4096]{0:T(1024)S(1)} %add_select_fusion, s32[4096]{0:T(1024)S(1)} %add_bitcast_fusion, s32[128]{0:T(128)S(1)} %get-tuple-element.55, s32[128]{0:T(128)S(1)} %get-tuple-element.56), kind=kOutput, calls=%fused_computation.24 | convolution fusion | flops 203952128 | bytes 1082368 | tf_op jit(solution)/shard_map/dot_general | solution.py:146
  76.3 2.0 %constant_dynamic-update-slice_fusion.14 = bf16[32,128,5,128]{3,1,0,2:T(8,128)(2,1)} fusion(bf16[32,128,5,128]{3,1,0,2:T(8,128)(2,1)} %get-tuple-element.20, bf16[16,128,5,128]{3,1,0,2:T(8,128)(2,1)S(1)} %collective-permute-done.8), kind=kLoop, calls=%fused_computation.73 | loop fusion | bytes 5242880 | tf_op jit(solution)/shard_map/concatenate | solution.py:88
  78.3 1.7 fusion.7
  80.0 2.7 %fusion.62 = (f32[128]{0:T(128)S(1)}, f32[128,4096]{1,0:T(8,128)S(1)}) fusion(pred[128,4096]{1,0:T(32,128)(4,1)S(1)} %fusion.12, f32[128,4096]{1,0:T(8,128)S(1)} %fusion.7, f32[128,16]{0,1:T(8,128)S(1)} %fusion.37, bf16[4096,5,128]{2,0,1:T(8,128)(2,1)} %bitcast.23), kind=kOutput, calls=%fused_computation.156 | convolution fusion | flops 102236032 | bytes 5775872 | tf_op jit(solution)/shard_map/dot_general | solution.py:127
  82.7 0.6 fusion.14
  83.3 2.1 %multiply_reduce_fusion = (f32[128]{0:T(128)S(1)}, bf16[128,128]{0,1:T(8,128)(2,1)S(1)}) fusion(bf16[128,128]{0,1:T(8,128)(2,1)S(1)} %copy.30, f32[128]{0:T(128)S(1)} %fusion.14, bf16[4096,5,128]{2,0,1:T(8,128)(2,1)} %bitcast.23, pred[128,4096]{1,0:T(32,128)(4,1)S(1)} %fusion.12, f32[128,4096]{1,0:T(8,128)S(1)} %get-tuple-element.52, ...), kind=kOutput, calls=%fused_computation.95 | convolution fusion | flops 135888768 | bytes 3737088 | tf_op jit(solution)/shard_map/dot_general | solution.py:133
  85.4 2.5 %collective-permute-start.9 = (f32[1,2,128]{2,1,0:T(2,128)S(1)}, f32[1,2,128]{2,1,0:T(2,128)S(1)}, u32[]{:S(2)}, u32[]{:S(2)}) collective-permute-start(f32[1,2,128]{2,1,0:T(2,128)S(1)} %maximum_bitcast_fusion), channel_id=1, source_target_pairs={{0,24},{24,0},{48,72},{72,48},{96,120},{120,96},{144,168},{168,144... | collective-permute-start | bytes 3080 | tf_op jit(solution)/shard_map/ppermute | solution.py:27
  88.0 0.8 collective-permute-done.9
  88.8 1.9 %collective-permute-start.10 = (f32[2,2,128]{2,1,0:T(2,128)S(1)}, f32[2,2,128]{2,1,0:T(2,128)S(1)}, u32[]{:S(2)}, u32[]{:S(2)}) collective-permute-start(f32[2,2,128]{2,1,0:T(2,128)S(1)} %pad_maximum_fusion.6), channel_id=1, source_target_pairs={{0,48},{24,72},{48,0},{72,24},{96,144},{120,168},{144,96},{168,120... | collective-permute-start | bytes 6152 | tf_op jit(solution)/shard_map/ppermute | solution.py:27
  90.7 3.5 %collective-permute-done.10 = f32[2,2,128]{2,1,0:T(2,128)S(1)} collective-permute-done((f32[2,2,128]{2,1,0:T(2,128)S(1)}, f32[2,2,128]{2,1,0:T(2,128)S(1)}, u32[]{:S(2)}, u32[]{:S(2)}) %collective-permute-start.10) | collective-permute-done | bytes 2080 | tf_op jit(solution)/shard_map/ppermute | solution.py:27
  94.3 2.2 %collective-permute-start.11 = (f32[4,2,128]{2,1,0:T(2,128)S(1)}, f32[4,2,128]{2,1,0:T(2,128)S(1)}, u32[]{:S(2)}, u32[]{:S(2)}) collective-permute-start(f32[4,2,128]{2,1,0:T(2,128)S(1)} %pad_maximum_fusion.5), channel_id=1, source_target_pairs={{0,96},{24,120},{48,144},{72,168},{96,0},{120,24},{144,48},{168,72... | collective-permute-start | bytes 12296 | tf_op jit(solution)/shard_map/ppermute | solution.py:27
  96.5 4.2 %collective-permute-done.11 = f32[4,2,128]{2,1,0:T(2,128)S(1)} collective-permute-done((f32[4,2,128]{2,1,0:T(2,128)S(1)}, f32[4,2,128]{2,1,0:T(2,128)S(1)}, u32[]{:S(2)}, u32[]{:S(2)}) %collective-permute-start.11) | collective-permute-done | bytes 4128 | tf_op jit(solution)/shard_map/ppermute | solution.py:27
  100.7 6.8 %collective-permute-start.12 = (f32[8,2,128]{2,1,0:T(2,128)S(1)}, f32[8,2,128]{2,1,0:T(2,128)S(1)}, u32[]{:S(2)}, u32[]{:S(2)}) collective-permute-start(f32[8,2,128]{2,1,0:T(2,128)S(1)} %pad_maximum_fusion.4), channel_id=1, source_target_pairs={{0,192},{24,216},{48,240},{72,264},{96,288},{120,312},{144,336},{1... | collective-permute-start | bytes 24584 | tf_op jit(solution)/shard_map/ppermute | solution.py:27
  107.4 2.7 %collective-permute-done.12 = f32[8,2,128]{2,1,0:T(2,128)S(1)} collective-permute-done((f32[8,2,128]{2,1,0:T(2,128)S(1)}, f32[8,2,128]{2,1,0:T(2,128)S(1)}, u32[]{:S(2)}, u32[]{:S(2)}) %collective-permute-start.12) | collective-permute-done | bytes 8224 | tf_op jit(solution)/shard_map/ppermute | solution.py:27
  110.1 9.5 %collective-permute-start.13 = (f32[16,2,128]{2,1,0:T(2,128)S(1)}, f32[16,2,128]{2,1,0:T(2,128)S(1)}, u32[]{:S(2)}, u32[]{:S(2)}) collective-permute-start(f32[16,2,128]{2,1,0:T(2,128)S(1)} %get-tuple-element.39), channel_id=1, source_target_pairs={{0,384},{24,408},{48,432},{72,456},{96,480},{120,504},{144,528},{1... | collective-permute-start | bytes 49160 | tf_op jit(solution)/shard_map/ppermute | solution.py:27
  119.7 3.1 %convolution_multiply_fusion = f32[4096,128]{0,1:T(8,128)} fusion(bf16[4096,5,128]{2,0,1:T(8,128)(2,1)} %bitcast.23, bf16[128,768]{1,0:T(8,128)(2,1)} %param.10, s32[]{:T(128)S(6)} %select_n.144), kind=kOutput, calls=%fused_computation.9 | convolution fusion | flops 134742016 | bytes 3178500 | tf_op jit(solution)/shard_map/dot_general | solution.py:151
  122.7 0.6 gather_fusion.1
  123.4 0.6 gather_fusion.2
  124.2 3.4 %fusion.3 = f32[4096,128]{0,1:T(8,128)S(1)} fusion(pred[4096,128]{0,1:T(32,128)(4,1)S(1)} %copy-done.2, f32[4096,128]{0,1:T(8,128)} %convolution_multiply_fusion, f32[128,16]{0,1:T(8,128)S(1)} %fusion.36, f32[4096]{0:T(1024)S(1)} %bitcast.134, bf16[4096,5,128]{2,0,1:T(8,128)(2,1)} %bitcast.23), kind=kOutput, calls=%fused_computation.8 | convolution fusion | flops 102236160 | bytes 5791744 | tf_op jit(solution)/shard_map/dot_general | solution.py:150
  127.6 1.7 convolution_bitcast_fusion
  129.3 2.3 %fusion.19 = f32[1,128,128]{2,1,0:T(8,128)S(1)} fusion(f32[4096,128]{0,1:T(8,128)S(1)} %fusion.3, f32[4096]{0:T(1024)S(1)} %bitcast.133, bf16[4096,5,128]{2,0,1:T(8,128)(2,1)} %bitcast.23, bf16[128,768]{1,0:T(8,128)(2,1)} %param.11, s32[]{:T(128)S(6)} %select_n.144), kind=kOutput, calls=%fused_computation.33 | convolution fusion | flops 270024704 | bytes 4308996 | tf_op jit(solution)/shard_map/dot_general | solution.py:155
  131.6 3.1 %collective-permute-start.14 = (f32[2,128,128]{2,1,0:T(8,128)S(1)}, f32[2,128,128]{2,1,0:T(8,128)S(1)}, u32[]{:S(2)}, u32[]{:S(2)}) collective-permute-start(f32[2,128,128]{2,1,0:T(8,128)S(1)} %pad_maximum_fusion.2), channel_id=1, source_target_pairs={{0,1},{1,0},{2,3},{3,2},{4,5},{5,4},{6,7},{7,6},{8,9},{9,8},{10,11... | collective-permute-start | bytes 393224 | tf_op jit(solution)/shard_map/ppermute | solution.py:36
  134.7 3.8 %collective-permute-done.14 = f32[2,128,128]{2,1,0:T(8,128)S(1)} collective-permute-done((f32[2,128,128]{2,1,0:T(8,128)S(1)}, f32[2,128,128]{2,1,0:T(8,128)S(1)}, u32[]{:S(2)}, u32[]{:S(2)}) %collective-permute-start.14) | collective-permute-done | bytes 131104 | tf_op jit(solution)/shard_map/ppermute | solution.py:36
  138.5 5.2 %collective-permute-start.15 = (f32[2,128,128]{2,1,0:T(8,128)S(1)}, f32[2,128,128]{2,1,0:T(8,128)S(1)}, u32[]{:S(2)}, u32[]{:S(2)}) collective-permute-start(f32[2,128,128]{2,1,0:T(8,128)S(1)} %fusion.59), channel_id=1, source_target_pairs={{0,2},{1,3},{2,0},{3,1},{4,6},{5,7},{6,4},{7,5},{8,10},{9,11},{10,... | collective-permute-start | bytes 393224 | tf_op jit(solution)/shard_map/ppermute | solution.py:36
  143.8 3.1 %collective-permute-done.15 = f32[2,128,128]{2,1,0:T(8,128)S(1)} collective-permute-done((f32[2,128,128]{2,1,0:T(8,128)S(1)}, f32[2,128,128]{2,1,0:T(8,128)S(1)}, u32[]{:S(2)}, u32[]{:S(2)}) %collective-permute-start.15) | collective-permute-done | bytes 131104 | tf_op jit(solution)/shard_map/ppermute | solution.py:36
  146.9 14.2 %collective-permute-start.16 = (bf16[1,2,128,128]{3,2,1,0:T(8,128)(2,1)S(1)}, bf16[1,2,128,128]{3,2,1,0:T(8,128)(2,1)S(1)}, u32[]{:S(2)}, u32[]{:S(2)}) collective-permute-start(bf16[1,2,128,128]{3,2,1,0:T(8,128)(2,1)S(1)} %fusion.34), channel_id=1, source_target_pairs={{0,20},{4,0},{8,4},{12,8},{16,12},{20,16},{1,21},{5,1},{9,5},{13,9... | collective-permute-start | bytes 196616 | tf_op jit(solution)/shard_map/ppermute | solution.py:49
  161.1 1.9 %collective-permute-done.16 = bf16[1,2,128,128]{3,2,1,0:T(8,128)(2,1)S(1)} collective-permute-done((bf16[1,2,128,128]{3,2,1,0:T(8,128)(2,1)S(1)}, bf16[1,2,128,128]{3,2,1,0:T(8,128)(2,1)S(1)}, u32[]{:S(2)}, u32[]{:S(2)}) %collective-permute-start.16) | collective-permute-done | bytes 65568 | tf_op jit(solution)/shard_map/ppermute | solution.py:49
  163.0 8.0 %collective-permute-start.17 = (bf16[2,2,128,128]{3,2,1,0:T(8,128)(2,1)S(1)}, bf16[2,2,128,128]{3,2,1,0:T(8,128)(2,1)S(1)}, u32[]{:S(2)}, u32[]{:S(2)}) collective-permute-start(bf16[2,2,128,128]{3,2,1,0:T(8,128)(2,1)S(1)} %pad_maximum_fusion.3), channel_id=1, source_target_pairs={{0,16},{4,20},{8,0},{12,4},{16,8},{20,12},{1,17},{5,21},{9,1},{13,... | collective-permute-start | bytes 393224 | tf_op jit(solution)/shard_map/ppermute | solution.py:49
  171.0 1.9 %collective-permute-start.18 = (bf16[2,2,128,128]{3,2,1,0:T(8,128)(2,1)S(1)}, bf16[2,2,128,128]{3,2,1,0:T(8,128)(2,1)S(1)}, u32[]{:S(2)}, u32[]{:S(2)}) collective-permute-start(bf16[2,2,128,128]{3,2,1,0:T(8,128)(2,1)S(1)} %pad_maximum_fusion.3), channel_id=1, source_target_pairs={{0,8},{4,12},{8,16},{12,20},{16,0},{20,4},{1,9},{5,13},{9,17},{13,... | collective-permute-start | bytes 393224 | tf_op jit(solution)/shard_map/ppermute | solution.py:49
  172.9 3.8 %fusion.21 = bf16[128,128]{1,0:T(8,128)(2,1)} fusion(bf16[128,128]{1,0:T(8,128)(2,1)S(1)} %copy-done.4, pred[128,4096]{1,0:T(32,128)(4,1)S(1)} %fusion.12, f32[128,4096]{1,0:T(8,128)} %copy-done.1, f32[128]{0:T(128)S(1)} %get-tuple-element.53, f32[128]{0:T(128)S(1)} %log_add_fusion, bf16[4096,5,128]{2,0,1:T(8,128)(2,1)} %bitcast.23), kind=kOutput, calls=%fused_computation.35 | convolution fusion | flops 271089664 | bytes 4785152 | tf_op jit(solution)/shard_map/dot_general | solution.py:140
  176.7 0.7 copy.38
  177.4 5.7 %collective-permute-done.18 = bf16[2,2,128,128]{3,2,1,0:T(8,128)(2,1)S(1)} collective-permute-done((bf16[2,2,128,128]{3,2,1,0:T(8,128)(2,1)S(1)}, bf16[2,2,128,128]{3,2,1,0:T(8,128)(2,1)S(1)}, u32[]{:S(2)}, u32[]{:S(2)}) %collective-permute-start.18) | collective-permute-done | bytes 131104 | tf_op jit(solution)/shard_map/ppermute | solution.py:49
  183.2 0.6 gather_fusion
  184.1 0.8 copy.39
  185.1 0.8 copy.40
  (65 shorter events, 2.8 us)
Async XLA Ops:
  0.6 70.8 %copy-start = (f32[1,16,16]{2,1,0:T(8,128)S(1)}, f32[1,16,16]{2,1,0:T(8,128)}, u32[]{:S(2)}) copy-start(f32[1,16,16]{2,1,0:T(8,128)} %param.13) | copy-start | bytes 3076
  4.5 19.5 %collective-permute-start = (bf16[1,128,5,128]{3,1,0,2:T(8,128)(2,1)S(1)}, bf16[1,128,5,128]{3,1,0,2:T(8,128)(2,1)S(1)}, u32[]{:S(2)}, u32[]{:S(2)}) collective-permute-start(bf16[1,128,5,128]{3,1,0,2:T(8,128)(2,1)S(1)} %bitcast.129), channel_id=1, source_target_pairs={{0,384},{384,0},{1,385},{385,1},{2,386},{386,2},{3,387},{387,3},{4... | collective-permute-start | bytes 491528 | tf_op jit(solution)/shard_map/ppermute | solution.py:69
  24.1 12.3 %collective-permute-start.1 = (bf16[2,128,5,128]{3,1,0,2:T(8,128)(2,1)S(1)}, bf16[2,128,5,128]{3,1,0,2:T(8,128)(2,1)S(1)}, u32[]{:S(2)}, u32[]{:S(2)}) collective-permute-start(bf16[2,128,5,128]{3,1,0,2:T(8,128)(2,1)S(1)} %pad_maximum_fusion.1), channel_id=1, source_target_pairs={{0,48},{48,96},{96,144},{144,192},{192,240},{240,288},{288,336},{3... | collective-permute-start | bytes 983048 | tf_op jit(solution)/shard_map/ppermute | solution.py:76
  28.3 10.3 %collective-permute-start.2 = (bf16[2,128,5,128]{3,1,0,2:T(8,128)(2,1)S(1)}, bf16[2,128,5,128]{3,1,0,2:T(8,128)(2,1)S(1)}, u32[]{:S(2)}, u32[]{:S(2)}) collective-permute-start(bf16[2,128,5,128]{3,1,0,2:T(8,128)(2,1)S(1)} %pad_maximum_fusion.1), channel_id=1, source_target_pairs={{0,336},{48,0},{96,48},{144,96},{192,144},{240,192},{288,240},{336... | collective-permute-start | bytes 983048 | tf_op jit(solution)/shard_map/ppermute | solution.py:81
  36.4 11.2 %collective-permute-start.3 = (bf16[2,128,5,128]{3,1,0,2:T(8,128)(2,1)S(1)}, bf16[2,128,5,128]{3,1,0,2:T(8,128)(2,1)S(1)}, u32[]{:S(2)}, u32[]{:S(2)}) collective-permute-start(bf16[2,128,5,128]{3,1,0,2:T(8,128)(2,1)S(1)} %collective-permute-done.1), channel_id=1, source_target_pairs={{0,48},{48,96},{96,144},{144,192},{192,240},{240,288},{288,336},{3... | collective-permute-start | bytes 983048 | tf_op jit(solution)/shard_map/ppermute | solution.py:76
  38.6 12.8 %collective-permute-start.4 = (bf16[2,128,5,128]{3,1,0,2:T(8,128)(2,1)S(1)}, bf16[2,128,5,128]{3,1,0,2:T(8,128)(2,1)S(1)}, u32[]{:S(2)}, u32[]{:S(2)}) collective-permute-start(bf16[2,128,5,128]{3,1,0,2:T(8,128)(2,1)S(1)} %collective-permute-done.2), channel_id=1, source_target_pairs={{0,336},{48,0},{96,48},{144,96},{192,144},{240,192},{288,240},{336... | collective-permute-start | bytes 983048 | tf_op jit(solution)/shard_map/ppermute | solution.py:81
  47.6 10.3 %collective-permute-start.5 = (bf16[2,128,5,128]{3,1,0,2:T(8,128)(2,1)S(1)}, bf16[2,128,5,128]{3,1,0,2:T(8,128)(2,1)S(1)}, u32[]{:S(2)}, u32[]{:S(2)}) collective-permute-start(bf16[2,128,5,128]{3,1,0,2:T(8,128)(2,1)S(1)} %collective-permute-done.3), channel_id=1, source_target_pairs={{0,48},{48,96},{96,144},{144,192},{192,240},{240,288},{288,336},{3... | collective-permute-start | bytes 983048 | tf_op jit(solution)/shard_map/ppermute | solution.py:76
  51.4 19.6 %copy-start.4 = (bf16[128,128]{1,0:T(8,128)(2,1)S(1)}, bf16[128,128]{1,0:T(8,128)(2,1)}, u32[]{:S(2)}) copy-start(bf16[128,128]{1,0:T(8,128)(2,1)} %param.15) | copy-start | bytes 98308
  51.4 20.0 %copy-start.6 = (s32[128]{0:T(128)S(1)}, s32[128]{0:T(128)}, u32[]{:S(2)}) copy-start(s32[128]{0:T(128)} %param.12) | copy-start | bytes 1540
  51.4 20.5 %copy-start.5 = (s32[32,32]{1,0:T(8,128)S(1)}, s32[32,32]{1,0:T(8,128)}, u32[]{:S(2)}) copy-start(s32[32,32]{1,0:T(8,128)} %param.14) | copy-start | bytes 12292
  51.4 10.3 %collective-permute-start.6 = (bf16[2,128,5,128]{3,1,0,2:T(8,128)(2,1)S(1)}, bf16[2,128,5,128]{3,1,0,2:T(8,128)(2,1)S(1)}, u32[]{:S(2)}, u32[]{:S(2)}) collective-permute-start(bf16[2,128,5,128]{3,1,0,2:T(8,128)(2,1)S(1)} %collective-permute-done.4), channel_id=1, source_target_pairs={{0,336},{48,0},{96,48},{144,96},{192,144},{240,192},{288,240},{336... | collective-permute-start | bytes 983048 | tf_op jit(solution)/shard_map/ppermute | solution.py:81
  57.9 10.2 %collective-permute-start.7 = (bf16[2,128,5,128]{3,1,0,2:T(8,128)(2,1)S(1)}, bf16[2,128,5,128]{3,1,0,2:T(8,128)(2,1)S(1)}, u32[]{:S(2)}, u32[]{:S(2)}) collective-permute-start(bf16[2,128,5,128]{3,1,0,2:T(8,128)(2,1)S(1)} %collective-permute-done.5), channel_id=1, source_target_pairs={{0,48},{48,96},{96,144},{144,192},{192,240},{240,288},{288,336},{3... | collective-permute-start | bytes 983048 | tf_op jit(solution)/shard_map/ppermute | solution.py:76
  69.0 7.3 %collective-permute-start.8 = (bf16[16,128,5,128]{3,1,0,2:T(8,128)(2,1)}, bf16[16,128,5,128]{3,1,0,2:T(8,128)(2,1)S(1)}, u32[]{:S(2)}, u32[]{:S(2)}) collective-permute-start(bf16[16,128,5,128]{3,1,0,2:T(8,128)(2,1)} %get-tuple-element.19), channel_id=1, source_target_pairs={{0,24},{24,0},{1,25},{25,1},{2,26},{26,2},{3,27},{27,3},{4,28},{28... | collective-permute-start | bytes 7864328 | tf_op jit(solution)/shard_map/ppermute | solution.py:87
  76.3 2.0 %copy-start.3 = (bf16[128,128]{1,0:T(8,128)(2,1)S(1)}, bf16[128,128]{1,0:T(8,128)(2,1)}, u32[]{:S(2)}) copy-start(bf16[128,128]{1,0:T(8,128)(2,1)} %param.9) | copy-start | bytes 98308
  82.7 2.7 %copy-start.1 = (f32[128,4096]{1,0:T(8,128)}, f32[128,4096]{1,0:T(8,128)S(1)}, u32[]{:S(2)}) copy-start(f32[128,4096]{1,0:T(8,128)S(1)} %get-tuple-element.52) | copy-start | bytes 6291460
  85.4 38.8 %copy-start.2 = (pred[4096,128]{0,1:T(32,128)(4,1)S(1)}, pred[4096,128]{0,1:T(32,128)(4,1)}, u32[]{:S(2)}) copy-start(pred[4096,128]{0,1:T(32,128)(4,1)} %fusion.13) | copy-start | bytes 1572868
  85.4 3.3 %collective-permute-start.9 = (f32[1,2,128]{2,1,0:T(2,128)S(1)}, f32[1,2,128]{2,1,0:T(2,128)S(1)}, u32[]{:S(2)}, u32[]{:S(2)}) collective-permute-start(f32[1,2,128]{2,1,0:T(2,128)S(1)} %maximum_bitcast_fusion), channel_id=1, source_target_pairs={{0,24},{24,0},{48,72},{72,48},{96,120},{120,96},{144,168},{168,144... | collective-permute-start | bytes 3080 | tf_op jit(solution)/shard_map/ppermute | solution.py:27
  88.8 5.5 %collective-permute-start.10 = (f32[2,2,128]{2,1,0:T(2,128)S(1)}, f32[2,2,128]{2,1,0:T(2,128)S(1)}, u32[]{:S(2)}, u32[]{:S(2)}) collective-permute-start(f32[2,2,128]{2,1,0:T(2,128)S(1)} %pad_maximum_fusion.6), channel_id=1, source_target_pairs={{0,48},{24,72},{48,0},{72,24},{96,144},{120,168},{144,96},{168,120... | collective-permute-start | bytes 6152 | tf_op jit(solution)/shard_map/ppermute | solution.py:27
  94.3 6.4 %collective-permute-start.11 = (f32[4,2,128]{2,1,0:T(2,128)S(1)}, f32[4,2,128]{2,1,0:T(2,128)S(1)}, u32[]{:S(2)}, u32[]{:S(2)}) collective-permute-start(f32[4,2,128]{2,1,0:T(2,128)S(1)} %pad_maximum_fusion.5), channel_id=1, source_target_pairs={{0,96},{24,120},{48,144},{72,168},{96,0},{120,24},{144,48},{168,72... | collective-permute-start | bytes 12296 | tf_op jit(solution)/shard_map/ppermute | solution.py:27
  100.7 9.4 %collective-permute-start.12 = (f32[8,2,128]{2,1,0:T(2,128)S(1)}, f32[8,2,128]{2,1,0:T(2,128)S(1)}, u32[]{:S(2)}, u32[]{:S(2)}) collective-permute-start(f32[8,2,128]{2,1,0:T(2,128)S(1)} %pad_maximum_fusion.4), channel_id=1, source_target_pairs={{0,192},{24,216},{48,240},{72,264},{96,288},{120,312},{144,336},{1... | collective-permute-start | bytes 24584 | tf_op jit(solution)/shard_map/ppermute | solution.py:27
  110.1 12.6 %collective-permute-start.13 = (f32[16,2,128]{2,1,0:T(2,128)S(1)}, f32[16,2,128]{2,1,0:T(2,128)S(1)}, u32[]{:S(2)}, u32[]{:S(2)}) collective-permute-start(f32[16,2,128]{2,1,0:T(2,128)S(1)} %get-tuple-element.39), channel_id=1, source_target_pairs={{0,384},{24,408},{48,432},{72,456},{96,480},{120,504},{144,528},{1... | collective-permute-start | bytes 49160 | tf_op jit(solution)/shard_map/ppermute | solution.py:27
  131.6 6.9 %collective-permute-start.14 = (f32[2,128,128]{2,1,0:T(8,128)S(1)}, f32[2,128,128]{2,1,0:T(8,128)S(1)}, u32[]{:S(2)}, u32[]{:S(2)}) collective-permute-start(f32[2,128,128]{2,1,0:T(8,128)S(1)} %pad_maximum_fusion.2), channel_id=1, source_target_pairs={{0,1},{1,0},{2,3},{3,2},{4,5},{5,4},{6,7},{7,6},{8,9},{9,8},{10,11... | collective-permute-start | bytes 393224 | tf_op jit(solution)/shard_map/ppermute | solution.py:36
  138.5 8.4 %collective-permute-start.15 = (f32[2,128,128]{2,1,0:T(8,128)S(1)}, f32[2,128,128]{2,1,0:T(8,128)S(1)}, u32[]{:S(2)}, u32[]{:S(2)}) collective-permute-start(f32[2,128,128]{2,1,0:T(8,128)S(1)} %fusion.59), channel_id=1, source_target_pairs={{0,2},{1,3},{2,0},{3,1},{4,6},{5,7},{6,4},{7,5},{8,10},{9,11},{10,... | collective-permute-start | bytes 393224 | tf_op jit(solution)/shard_map/ppermute | solution.py:36
  146.9 16.1 %collective-permute-start.16 = (bf16[1,2,128,128]{3,2,1,0:T(8,128)(2,1)S(1)}, bf16[1,2,128,128]{3,2,1,0:T(8,128)(2,1)S(1)}, u32[]{:S(2)}, u32[]{:S(2)}) collective-permute-start(bf16[1,2,128,128]{3,2,1,0:T(8,128)(2,1)S(1)} %fusion.34), channel_id=1, source_target_pairs={{0,20},{4,0},{8,4},{12,8},{16,12},{20,16},{1,21},{5,1},{9,5},{13,9... | collective-permute-start | bytes 196616 | tf_op jit(solution)/shard_map/ppermute | solution.py:49
  163.0 14.5 %collective-permute-start.17 = (bf16[2,2,128,128]{3,2,1,0:T(8,128)(2,1)S(1)}, bf16[2,2,128,128]{3,2,1,0:T(8,128)(2,1)S(1)}, u32[]{:S(2)}, u32[]{:S(2)}) collective-permute-start(bf16[2,2,128,128]{3,2,1,0:T(8,128)(2,1)S(1)} %pad_maximum_fusion.3), channel_id=1, source_target_pairs={{0,16},{4,20},{8,0},{12,4},{16,8},{20,12},{1,17},{5,21},{9,1},{13,... | collective-permute-start | bytes 393224 | tf_op jit(solution)/shard_map/ppermute | solution.py:49
  171.0 12.2 %collective-permute-start.18 = (bf16[2,2,128,128]{3,2,1,0:T(8,128)(2,1)S(1)}, bf16[2,2,128,128]{3,2,1,0:T(8,128)(2,1)S(1)}, u32[]{:S(2)}, u32[]{:S(2)}) collective-permute-start(bf16[2,2,128,128]{3,2,1,0:T(8,128)(2,1)S(1)} %pad_maximum_fusion.3), channel_id=1, source_target_pairs={{0,8},{4,12},{8,16},{12,20},{16,0},{20,4},{1,9},{5,13},{9,17},{13,... | collective-permute-start | bytes 393224 | tf_op jit(solution)/shard_map/ppermute | solution.py:49
